TPU v7x, 128 devices: a whole 4x4x4 slice. The times are simulated.
128 devices in a mesh: row: 4 (over z_lo, core), col: 4 (over x), slab: 8 (over y, z_hi).
Axes of the slice: x: 4, y: 4, z: 4 (z_hi: 2, z_lo: 2; z = z_hi * 2 + z_lo), core: 2. Of those that a mesh axis runs over, the one named last changes fastest.
Arguments:
- amplitudes: bfloat16 [48, 48, 480, 128], P('row', 'col', 'slab'), may hold values from -6 to 6
- integrals: bfloat16 [48, 480, 48, 128], P('row', 'slab', 'col'), may hold values from -0.0625 to 0.0625
- irreps: int32 [19], replicated, may hold values from 0 to 1
- pair_mask: int32 [4, 4], replicated, may hold values 0 or 1
Outputs:
- cycle_term: bfloat16 [48, 48, 128, 128], P('row', 'col', 'slab')
Inputs may be any that keep to these rules, and one draw needn't show every extreme that they name: Each label is one of the two irreps of the point group. `pair_mask`: 1 marks a block pair whose amplitudes are kept.
All inputs are finite; a program needn't handle non-finite values.
Results may differ from a plain program's by a relative error of at most 0.001.
Values may be sent and summed in bfloat16 or wider, within the bound.
No kernel may reach another device: no remote copies, remote signals or barrier semaphores. Data moves between devices by JAX's collectives and lax.ppermute only.
A program may use at most 128 MiB of HBM per device.

v0:
```python
import jax
import jax.numpy as jnp
from jax import lax
from jax.sharding import PartitionSpec as P

OBLK = 12
VTILE = 32


def swapped(value, axis, stride):
    mask = 2**stride
    pairs = [(source, source ^ mask) for source in range(lax.axis_size(axis))]
    return lax.ppermute(value, axis, pairs)


def block_onehot(first_row, row_count, blocks, block_width):
    block_ids = (first_row + jnp.arange(row_count, dtype=jnp.int32)) // block_width
    return (block_ids[:, None] == jnp.arange(blocks, dtype=jnp.int32)[None, :]).astype(jnp.float32)


def contract(amp_piece, int_piece, i_start, k_start, pair_mask):
    i_rows = amp_piece.shape[0]
    k_count = amp_piece.shape[1]
    blocks = pair_mask.shape[0]
    factor = jnp.dot(
        jnp.dot(block_onehot(i_start, i_rows, blocks, OBLK), pair_mask.astype(jnp.float32)),
        block_onehot(k_start, k_count, blocks, OBLK).T,
    )
    masked = amp_piece * factor.astype(jnp.bfloat16)[:, :, None, None]
    return jnp.einsum("ikca,kcjb->ijab", masked, int_piece, preferred_element_type=jnp.float32)


def body(amplitudes, integrals, irreps, pair_mask):
    i_rows, k_rows, c_cols, win_cols = amplitudes.shape
    j_rows = integrals.shape[2]
    blocks = pair_mask.shape[0]
    row_at = lax.axis_index("row")
    col_at = lax.axis_index("col")
    slab_at = lax.axis_index("slab")
    i_start = row_at * i_rows
    occ_labels = irreps[:blocks].astype(jnp.float32)
    vir_labels = irreps[blocks:].astype(jnp.float32)
    vir_tiles = vir_labels.shape[0]
    label_k = jnp.dot(
        block_onehot(row_at * integrals.shape[0], integrals.shape[0], blocks, OBLK), occ_labels
    )
    label_c = jnp.dot(block_onehot(slab_at * c_cols, c_cols, vir_tiles, VTILE), vir_labels)
    label_j = jnp.dot(block_onehot(col_at * j_rows, j_rows, blocks, OBLK), occ_labels)
    label_b = jnp.dot(block_onehot(0, win_cols, vir_tiles, VTILE), vir_labels)
    parity = (
        label_k[:, None, None, None]
        + label_c[None, :, None, None]
        + label_j[None, None, :, None]
        + label_b[None, None, None, :]
    )
    screened = jnp.where(jnp.remainder(parity, 2.0) == 0.0, integrals, jnp.zeros_like(integrals))
    int_whole = lax.all_gather(screened, "row", axis=0, tiled=True)
    cycle_part = contract(
        lax.all_gather(amplitudes, "col", axis=1, tiled=True),
        int_whole,
        i_start,
        jnp.int32(0),
        pair_mask,
    )
    shares = lax.psum_scatter(cycle_part, "slab", scatter_dimension=2, tiled=True)
    spread = lax.all_to_all(shares, "slab", split_axis=3, concat_axis=2, tiled=True)
    mirrored = jnp.transpose(spread, (1, 0, 3, 2))
    for bit_no in range(lax.axis_size("row").bit_length() - 1):
        across = swapped(swapped(mirrored, "row", bit_no), "col", bit_no)
        differ = row_at // 2**bit_no % 2 != col_at // 2**bit_no % 2
        mirrored = jnp.where(differ, across, mirrored)
    return (shares + mirrored).astype(jnp.bfloat16)


def solution(mesh):
    return jax.shard_map(
        body,
        mesh=mesh,
        in_specs=(P("row", "col", "slab", None), P("row", "slab", "col", None), P(), P()),
        out_specs=P("row", "col", "slab", None),
        check_vma=False,
    )
```

profile of v0, /device:TPU:0, one launch (start us, length us, event | category | flops | bytes accessed | tf_op | source)
XLA Modules:
  0.0 556.6 jit_solution(18274877579923600509)
XLA Ops:
  6.5 0.7 all-gather.5.cloned.1.call-update
  7.4 0.2 convolution_bitcast_fusion
  7.6 0.2 convolution_bitcast_fusion.1
  7.8 0.2 convolution_bitcast_fusion.2
  8.0 0.2 convolution_bitcast_fusion.3
  8.4 5.2 fusion.9
  13.7 0.6 copy-done.1
  14.3 0.4 convolution_convert_fusion
  14.6 88.8 %all-gather.5.cloned.1.call-done = bf16[12,48,60,128]{3,2,1,0:T(8,128)(2,1)} async-done(((bf16[12,12,60,128]{3,2,1,0:T(8,128)(2,1)}), bf16[12,48,60,128]{3,2,1,0:T(8,128)(2,1)}) %all-gather.5.cloned.1.call-update) | async-done | bytes 8847376 | tf_op jit(solution)/shard_map/all_gather | solution.py:59
  103.4 91.3 %all-gather.3.cloned.1.call-done = bf16[48,60,12,128]{3,1,0,2:T(8,128)(2,1)} async-done(((bf16[12,60,12,128]{3,1,0,2:T(8,128)(2,1)}), bf16[48,60,12,128]{3,1,0,2:T(8,128)(2,1)}) %all-gather.3.cloned.1.call-update) | async-done | bytes 8847376 | tf_op jit(solution)/shard_map/all_gather | solution.py:57
  194.7 21.9 %fusion.10 = f32[12,12,128,128]{2,3,0,1:T(8,128)} fusion(bf16[12,48,60,128]{3,2,1,0:T(8,128)(2,1)} %all-gather.5.cloned.1.call-done, bf16[12,48]{1,0:T(8,128)(2,1)S(1)} %convolution_convert_fusion, bf16[48,60,12,128]{3,1,0,2:T(8,128)(2,1)} %all-gather.3.cloned.1.call-done), kind=kOutput, calls=%fused_computation.13 | convolution fusion | flops 13607239680 | bytes 27133056 | tf_op jit(solution)/shard_map/ikca,kcjb->ijab/dot_general | solution.py:30
  216.6 12.7 %copy.18 = f32[12,12,128,128]{3,1,0,2:T(8,128)} copy(f32[12,12,128,128]{2,3,0,1:T(8,128)} %fusion.10) | data formatting | bytes 18874368 | tf_op jit(solution)/shard_map/ikca,kcjb->ijab/transpose | solution.py:30
  229.3 153.7 %reduce-scatter.2.cloned.1.call-done = f32[12,12,16,128]{3,1,0,2:T(8,128)} async-done(((f32[12,12,128,128]{3,1,0,2:T(8,128)}), f32[12,12,16,128]{3,1,0,2:T(8,128)}) %reduce-scatter.2.cloned.1.call-update) | async-done | bytes 1179664 | tf_op jit(solution)/shard_map/reduce_scatter | solution.py:65
  383.1 14.2 %copy.19 = f32[12,12,16,128]{2,0,1,3:T(8,128)} copy(f32[12,12,16,128]{3,1,0,2:T(8,128)} %reduce-scatter.2.cloned.1.call-done) | data formatting | bytes 2359296 | tf_op jit(solution)/shard_map/reduce_scatter | solution.py:65
  397.3 8.8 %reshape.121 = f32[8,1,36864]{2,1,0:T(1,128)S(1)} reshape(f32[128,12,12,16]{3,2,1,0:T(8,128)} %bitcast.47) | data formatting | bytes 2359296
  406.1 20.4 %all_to_all.18 = f32[8,1,36864]{2,1,0:T(1,128)S(1)} all-to-all(f32[8,1,36864]{2,1,0:T(1,128)S(1)} %reshape.121), channel_id=1, replica_groups=mesh['row'=4,'col'=4,'slab'=8] {'slab'}, dimensions={0} | all-to-all | bytes 2359296 | tf_op jit(solution)/shard_map/all_to_all | solution.py:66
  426.5 0.5 broadcast.211
  427.0 3.4 reduce
  430.5 10.0 %reshape.122 = f32[128,12,12,16]{3,2,1,0:T(8,128)} reshape(f32[8,36864]{1,0:T(8,128)S(1)} %reduce) | data formatting | bytes 2359296
  440.5 13.8 %copy.38 = f32[12,12,16,8,16]{2,3,4,1,0:T(8,128)} copy(f32[12,12,16,8,16]{2,0,1,4,3:T(8,128)} %bitcast.48) | data formatting | bytes 2359296 | tf_op jit(solution)/shard_map/all_to_all | solution.py:66
  454.3 6.2 %all_to_all.16 = f32[12,12,128,16]{2,3,1,0:T(8,128)S(1)} reshape(f32[12,12,8,16,16]{3,2,4,1,0:T(8,128)} %bitcast.49) | data formatting | bytes 2359296 | tf_op jit(solution)/shard_map/all_to_all | solution.py:66
  460.5 0.1 copy.21
  460.8 2.8 collective-permute-done
  463.6 1.5 collective-permute-start.1
  465.1 26.5 %collective-permute-done.1 = f32[12,12,16,128]{3,2,1,0:T(8,128)S(1)} collective-permute-done((f32[12,12,16,128]{3,2,1,0:T(8,128)S(1)}, f32[12,12,16,128]{3,2,1,0:T(8,128)S(1)}, u32[]{:S(2)}, u32[]{:S(2)}) %collective-permute-start.1) | collective-permute-done | bytes 1179680 | tf_op jit(solution)/shard_map/ppermute | solution.py:13
  491.6 0.2 copy_select_fusion.1
  491.9 1.3 collective-permute-start.2
  493.2 25.9 %collective-permute-done.2 = f32[12,12,16,128]{3,2,1,0:T(8,128)S(1)} collective-permute-done((f32[12,12,16,128]{3,2,1,0:T(8,128)S(1)}, f32[12,12,16,128]{3,2,1,0:T(8,128)S(1)}, u32[]{:S(2)}, u32[]{:S(2)}) %collective-permute-start.2) | collective-permute-done | bytes 1179680 | tf_op jit(solution)/shard_map/ppermute | solution.py:13
  519.1 3.0 collective-permute-start.3
  522.1 24.8 %collective-permute-done.3 = f32[12,12,16,128]{3,2,1,0:T(8,128)S(1)} collective-permute-done((f32[12,12,16,128]{3,2,1,0:T(8,128)S(1)}, f32[12,12,16,128]{3,2,1,0:T(8,128)S(1)}, u32[]{:S(2)}, u32[]{:S(2)}) %collective-permute-start.3) | collective-permute-done | bytes 1179680 | tf_op jit(solution)/shard_map/ppermute | solution.py:13
  546.9 2.2 fusion.15
  549.1 1.0 copy.26
  (19 shorter events, 0.6 us)
Async XLA Ops:
  6.5 0.9 copy-start.2
  6.5 1.8 copy-start
  6.5 96.9 %all-gather.5.cloned.1.call-start = ((), (), s32[]{:S(2)}) async-start(), calls=%async_computation.3 | async-start | bytes 11796480 | tf_op jit(solution)/shard_map/all_gather | solution.py:59
  7.3 187.4 %all-gather.3.cloned.1.call-start = ((), (), s32[]{:S(2)}) async-start(), calls=%async_computation.2 | async-start | bytes 11796480 | tf_op jit(solution)/shard_map/all_gather | solution.py:57
  13.6 0.7 copy-start.1
  13.6 369.5 %reduce-scatter.2.cloned.1.call-start = ((), (), s32[]{:S(2)}) async-start(), calls=%async_computation.4 | async-start | bytes 14155776 | tf_op jit(solution)/shard_map/reduce_scatter | solution.py:65
  460.7 2.9 collective-permute-start
  463.6 28.0 %collective-permute-start.1 = (f32[12,12,16,128]{3,2,1,0:T(8,128)S(1)}, f32[12,12,16,128]{3,2,1,0:T(8,128)S(1)}, u32[]{:S(2)}, u32[]{:S(2)}) collective-permute-start(f32[12,12,16,128]{3,2,1,0:T(8,128)S(1)} %collective-permute-done), channel_id=1, source_target_pairs={{0,8},{8,0},{16,24},{24,16},{1,9},{9,1},{17,25},{25,17},{2,10},{10... | collective-permute-start | bytes 3538952 | tf_op jit(solution)/shard_map/ppermute | solution.py:13
  491.9 27.2 %collective-permute-start.2 = (f32[12,12,16,128]{3,2,1,0:T(8,128)S(1)}, f32[12,12,16,128]{3,2,1,0:T(8,128)S(1)}, u32[]{:S(2)}, u32[]{:S(2)}) collective-permute-start(f32[12,12,16,128]{3,2,1,0:T(8,128)S(1)} %copy.23), channel_id=1, source_target_pairs={{0,64},{32,96},{64,0},{96,32},{1,65},{33,97},{65,1},{97,33},{2,66}... | collective-permute-start | bytes 3538952 | tf_op jit(solution)/shard_map/ppermute | solution.py:13
  519.1 27.8 %collective-permute-start.3 = (f32[12,12,16,128]{3,2,1,0:T(8,128)S(1)}, f32[12,12,16,128]{3,2,1,0:T(8,128)S(1)}, u32[]{:S(2)}, u32[]{:S(2)}) collective-permute-start(f32[12,12,16,128]{3,2,1,0:T(8,128)S(1)} %collective-permute-done.2), channel_id=1, source_target_pairs={{0,16},{8,24},{16,0},{24,8},{1,17},{9,25},{17,1},{25,9},{2,18},{10... | collective-permute-start | bytes 3538952 | tf_op jit(solution)/shard_map/ppermute | solution.py:13
Sparse Core Ops, SparseCore 0:
  9.0 94.3 all-gather.4
  105.1 89.5 all-gather.2
  229.4 153.5 reduce-scatter.1
where the time goes:
time: 557 us
  waiting for transfers between devices  415 us (75%)
  local copies, waits for them, and re-layouts  68.1 us (12%)
  matrix products  23.1 us (4%)
  blocking collectives  20.4 us (4%)
  between operations  13.2 us (2%)
  other arithmetic  11.2 us (2%)
  starting transfers between devices  6.01 us (1%)
    reduce_scatter x1, waiting for transfers between devices, body(): lax.psum_scatter(cycle_part, 'slab', scatter_dimension=2, tiled=True)  154 us
    all_gather x1, waiting for transfers between devices, body(): int_whole = lax.all_gather(screened, 'row', axis=0, tiled=True)  91.3 us
    all_gather x1, waiting for transfers between devices, body(): lax.all_gather(amplitudes, 'col', axis=1, tiled=True)  88.8 us
    ppermute x4, waiting for transfers between devices, swapped(): return lax.ppermute(value, axis, pairs)  80 us
    dot_general x1, matrix products, contract(): jnp.einsum('ikca,kcjb->ijab', masked, int_piece, preferred_element_type=j...  21.9 us
    all_to_all x3, local copies, waits for them, and re-layouts, body(): lax.all_to_all(shares, 'slab', split_axis=3, concat_axis=2, tiled=True)  20.5 us
    all_to_all x1, blocking collectives, body(): lax.all_to_all(shares, 'slab', split_axis=3, concat_axis=2, tiled=True)  20.4 us
    unnamed x8, local copies, waits for them, and re-layouts  19.5 us
  transfers between devices with their start and end apart: 7, of which 7 were waited for; matrix products, arithmetic and copies ran while one was open for 1% of the time, Pallas kernels for 0%

commit v1 on v0

v1 whole, which is shorter than its diff:
```python
import jax
import jax.numpy as jnp
from jax import lax
from jax.sharding import PartitionSpec as P

OBLK = 12
VTILE = 32


def shifted(value, axis, fn):
    size = lax.axis_size(axis)
    return lax.ppermute(value, axis, [(src, fn(src) % size) for src in range(size)])


def int_mask(irreps, blocks, row_at, col_at, slab_at, c_cols, win_cols):
    c_ids = slab_at * c_cols + jnp.arange(c_cols, dtype=jnp.int32)
    b_ids = jnp.arange(win_cols, dtype=jnp.int32)
    label_c = jnp.take(irreps, blocks + c_ids // VTILE)
    label_b = jnp.take(irreps, blocks + b_ids // VTILE)
    occ = irreps[row_at] + irreps[col_at]
    parity = occ + label_c[:, None] + label_b[None, :]
    return parity % 2 == 0


def gather_col(amp):
    near1 = shifted(amp, "col", lambda c: c ^ 1)
    near3 = shifted(amp, "col", lambda c: c ^ 3)
    half = amp.shape[0] // 2
    far_a = shifted(near3[:half], "col", lambda c: c ^ 1)
    far_b = shifted(near1[half:], "col", lambda c: c ^ 3)
    far = jnp.concatenate([far_a, far_b], axis=0)
    return [amp, near1, far, near3]


def gather_row(ints):
    zpart = shifted(ints, "row", lambda r: r ^ 2)
    pair = jnp.stack([ints, zpart])
    other = shifted(pair, "row", lambda r: r ^ 1)
    return jnp.stack([ints, other[0], zpart, other[1]])


def ring_reduce_y(part, slab_at):
    ny = lax.axis_size("slab") // 2
    width = part.shape[2] // ny
    y_at = slab_at // 2
    half = part.shape[0] // 2
    halves = (part[:half], part[half:])
    dirs = (1, -1)
    acc = [None, None]
    for step in range(ny - 1):
        for h in range(2):
            d = dirs[h]
            chunk = (y_at - d * (step + 1)) % ny
            own = lax.dynamic_slice_in_dim(halves[h], chunk * width, width, axis=2)
            send = own if acc[h] is None else acc[h] + own
            acc[h] = shifted(send, "slab", lambda s, d=d: s + 2 * d)
    result = []
    for h in range(2):
        own = lax.dynamic_slice_in_dim(halves[h], y_at * width, width, axis=2)
        result.append(acc[h] + own)
    return jnp.concatenate(result, axis=0)


def body(amplitudes, integrals, irreps, pair_mask):
    i_rows, k_rows, c_cols, win_cols = amplitudes.shape
    blocks = pair_mask.shape[0]
    row_at = lax.axis_index("row")
    col_at = lax.axis_index("col")
    slab_at = lax.axis_index("slab")
    n_slab = lax.axis_size("slab")

    keep = pair_mask[row_at, col_at] != 0
    amp = jnp.where(keep, amplitudes, jnp.zeros_like(amplitudes))
    mask = int_mask(irreps, blocks, row_at, col_at, slab_at, c_cols, win_cols)
    ints = jnp.where(mask[None, :, None, :], integrals, jnp.zeros_like(integrals))

    amp_x = gather_col(amp)
    int_x = gather_row(ints)
    part = None
    for v in range(4):
        u = (col_at ^ v) ^ row_at
        int_blk = lax.dynamic_index_in_dim(int_x, u, axis=0, keepdims=False)
        term = jnp.einsum("ikca,kcjb->ijab", amp_x[v], int_blk, preferred_element_type=jnp.float32)
        part = term if part is None else part + term

    reduced_y = ring_reduce_y(part, slab_at)
    zh = slab_at % 2
    width = reduced_y.shape[2] // 2
    mine = lax.dynamic_slice_in_dim(reduced_y, zh * width, width, axis=2)
    theirs = lax.dynamic_slice_in_dim(reduced_y, (1 - zh) * width, width, axis=2)
    shares = mine + shifted(theirs, "slab", lambda s: s ^ 1)

    n_row = lax.axis_size("row")
    n_col = lax.axis_size("col")
    axes = ("row", "col", "slab")
    tiles = []
    for d in range(n_slab):
        dest_slab = slab_at ^ d
        tile = lax.dynamic_slice_in_dim(shares, dest_slab * width, width, axis=3)
        pairs = []
        for r in range(n_row):
            for c in range(n_col):
                for t in range(n_slab):
                    pairs.append(((r * n_col + c) * n_slab + t, (c * n_col + r) * n_slab + (t ^ d)))
        tiles.append(lax.ppermute(tile, axes, pairs))
    stacked = jnp.stack(tiles)
    order = jnp.arange(n_slab, dtype=jnp.int32) ^ slab_at
    ordered = jnp.take(stacked, order, axis=0)
    mirrored = jnp.transpose(ordered, (2, 1, 4, 0, 3)).reshape(shares.shape)
    return (shares + mirrored).astype(jnp.bfloat16)


def solution(mesh):
    return jax.shard_map(
        body,
        mesh=mesh,
        in_specs=(P("row", "col", "slab", None), P("row", "slab", "col", None), P(), P()),
        out_specs=P("row", "col", "slab", None),
        check_vma=False,
    )
```

time: 557 us -> 683 us (1.23)
  the two profiles are of different devices: /device:TPU:0 before, /device:TPU:52 now
where the time goes in v1:
time: 683 us; the launch traced here: 680 us
  waiting for transfers between devices  475 us (70%)
  local copies, waits for them, and re-layouts  87.7 us (13%)
  other arithmetic  41.7 us (6%)
  matrix products  40.5 us (6%)
  starting transfers between devices  32 us (5%)
    ppermute x8, waiting for transfers between devices, body(): tiles.append(lax.ppermute(tile, axes, pairs))  279 us
    ppermute x13, waiting for transfers between devices, shifted(): lax.ppermute(value, axis, [(src, fn(src) % size) for src in range(size)])  196 us
    dot_general x4, matrix products, body(): jnp.einsum('ikca,kcjb->ijab', amp_x[v], int_blk, preferred_element_type=j...  40.5 us
    ppermute x13, starting transfers between devices, shifted(): lax.ppermute(value, axis, [(src, fn(src) % size) for src in range(size)])  16.8 us
    ppermute x8, starting transfers between devices, body(): tiles.append(lax.ppermute(tile, axes, pairs))  15.3 us
    unnamed x19, local copies, waits for them, and re-layouts  14.3 us
  transfers between devices with their start and end apart: 21, of which 11 were waited for; matrix products, arithmetic and copies ran while one was open for 9% of the time, Pallas kernels for 0%

profile of v1, /device:TPU:52, one launch (start us, length us, event | category | flops | bytes accessed | tf_op | source)
XLA Modules:
  0.0 679.8 jit_solution(2255069348838380631)
XLA Ops:
  6.2 11.7 %and_select_fusion.1 = s32[128]{0:T(128)S(1)} fusion(s32[]{:T(128)} %bitcast.26, s32[]{:T(128)} %bitcast.27, s32[]{:T(128)} %bitcast.28, s32[]{:T(128)} %bitcast.29, s32[]{:T(128)} %bitcast.30, s32[]{:T(128)} %bitcast.32, s32[]{:T(128)} %bitcast.31, s32[]{:T(128)} %bitcast.3, s32[]{:T(128)} %bitcast.5, s32[]{:T(128)} %bitcast.7, s32[]{:T(128)} %bitcast.9, ...), kind=kLoop, calls=%fused_computation.99 | loop fusion | flops 8192 | bytes 588 | tf_op jit(solution)/shard_map/jit(_take)/select_n | solution.py:19
  20.6 52.5 %collective-permute-done = bf16[12,60,12,128]{3,1,2,0:T(8,128)(2,1)S(1)} collective-permute-done((bf16[12,60,12,128]{3,1,2,0:T(8,128)(2,1)S(1)}, bf16[12,60,12,128]{3,1,2,0:T(8,128)(2,1)S(1)}, u32[]{:S(2)}, u32[]{:S(2)}) %collective-permute-start) | collective-permute-done | bytes 2211872 | tf_op jit(solution)/shard_map/ppermute | solution.py:12
  74.5 2.6 pad_maximum_fusion.1
  77.1 9.0 %copy.24 = bf16[2,12,60,12,128]{4,0,3,2,1:T(2,128)(2,1)} copy(bf16[2,12,60,12,128]{4,2,3,1,0:T(8,128)(2,1)} %pad_maximum_fusion.1) | data formatting | bytes 8847360 | tf_op jit(solution)/shard_map/stack | solution.py:37
  90.1 2.8 collective-permute-start.2
  92.9 51.1 %collective-permute-done.3 = bf16[12,12,60,128]{3,2,1,0:T(8,128)(2,1)} collective-permute-done((bf16[12,12,60,128]{3,2,1,0:T(8,128)(2,1)}, bf16[12,12,60,128]{3,2,1,0:T(8,128)(2,1)}, u32[]{:S(2)}, u32[]{:S(2)}) %collective-permute-start.3) | collective-permute-done | bytes 2211872 | tf_op jit(solution)/shard_map/ppermute | solution.py:12
  151.0 10.2 %fusion.28 = (bf16[1,12,60,12,128]{4,0,3,2,1:T(2,128)(2,1)S(1)}, bf16[1,12,60,12,128]{4,0,3,2,1:T(2,128)(2,1)S(1)}) fusion(bf16[2,12,60,12,128]{4,0,3,2,1:T(2,128)(2,1)} %collective-permute-done.1), kind=kLoop, calls=%fused_computation.122 | loop fusion | bytes 8847360 | tf_op jit(solution)/shard_map/slice | solution.py:39
  164.9 5.7 constant_dynamic-slice_fusion.10
  170.6 10.0 %fusion.8 = f32[12,128,12,128,1]{1,3,4,2,0:T(8,128)} fusion(bf16[12,12,60,128]{3,2,1,0:T(8,128)(2,1)} %broadcast_select_fusion, bf16[1,12,60,12,128]{4,2,3,1,0:T(8,128)(2,1)} %get-tuple-element.10), kind=kOutput, calls=%fused_computation.21 | convolution fusion | flops 3397386240 | bytes 13860864 | tf_op jit(solution)/shard_map/ikca,kcjb->ijab/dot_general | solution.py:83
  180.6 8.0 %fusion.6 = f32[12,128,12,128,1]{1,3,4,2,0:T(8,128)} fusion(bf16[12,12,60,128]{3,2,1,0:T(8,128)(2,1)} %collective-permute-done.2, bf16[1,12,60,12,128]{4,2,3,1,0:T(8,128)(2,1)S(1)} %copy-done.4), kind=kOutput, calls=%fused_computation.19 | convolution fusion | flops 3397386240 | bytes 13860864 | tf_op jit(solution)/shard_map/ikca,kcjb->ijab/dot_general | solution.py:83
  188.6 8.2 %fusion.1 = f32[12,128,12,128,1]{1,3,4,2,0:T(8,128)} fusion(bf16[6,12,60,128]{3,2,1,0:T(8,128)(2,1)} %collective-permute-done.5, bf16[6,12,60,128]{3,2,1,0:T(8,128)(2,1)} %collective-permute-done.4, bf16[1,12,60,12,128]{4,2,3,1,0:T(8,128)(2,1)S(1)} %get-tuple-element.8), kind=kOutput, calls=%fused_computation.14 | convolution fusion | flops 3401809920 | bytes 13860864 | tf_op jit(solution)/shard_map/ikca,kcjb->ijab/dot_general | solution.py:83
  196.7 14.4 %fusion = f32[12,12,128,128]{3,2,0,1:T(8,128)} fusion(f32[12,128,12,128,1]{1,3,4,2,0:T(8,128)} %fusion.1, f32[12,128,12,128,1]{1,3,4,2,0:T(8,128)} %fusion.6, f32[12,128,12,128,1]{1,3,4,2,0:T(8,128)} %fusion.8, bf16[12,12,60,128]{3,2,1,0:T(8,128)(2,1)} %collective-permute-done.3, bf16[1,12,60,12,128]{4,2,3,1,0:T(8,128)(2,1)S(1)} %get-tuple-element.7), kind=kOutput, calls=%fused_computation.4 | convolution fusion | flops 3404464128 | bytes 42172416 | tf_op jit(solution)/shard_map/ikca,kcjb->ijab/dot_general | solution.py:83
  211.1 6.9 %fusion.27 = (f32[6,12,128,128]{3,2,0,1:T(8,128)S(1)}, f32[6,12,128,128]{3,2,0,1:T(8,128)}) fusion(f32[12,12,128,128]{3,2,0,1:T(8,128)} %fusion), kind=kLoop, calls=%fused_computation.121 | loop fusion | bytes 18874368 | tf_op jit(solution)/shard_map/slice | solution.py:47
  223.9 23.7 %collective-permute-done.9 = f32[6,12,32,128]{3,2,0,1:T(8,128)S(1)} collective-permute-done((f32[6,12,32,128]{3,2,0,1:T(8,128)S(1)}, f32[6,12,32,128]{3,2,0,1:T(8,128)S(1)}, u32[]{:S(2)}, u32[]{:S(2)}) %collective-permute-start.9) | collective-permute-done | bytes 1179680 | tf_op jit(solution)/shard_map/ppermute | solution.py:12
  253.8 22.6 %collective-permute-done.10 = f32[6,12,32,128]{3,2,0,1:T(8,128)S(1)} collective-permute-done((f32[6,12,32,128]{3,2,0,1:T(8,128)S(1)}, f32[6,12,32,128]{3,2,0,1:T(8,128)S(1)}, u32[]{:S(2)}, u32[]{:S(2)}) %collective-permute-start.10) | collective-permute-done | bytes 1179680 | tf_op jit(solution)/shard_map/ppermute | solution.py:12
  278.0 2.9 dynamic-slice_add_fusion.4
  280.9 2.9 collective-permute-start.8
  283.9 20.8 %collective-permute-done.11 = f32[6,12,32,128]{3,2,0,1:T(8,128)S(1)} collective-permute-done((f32[6,12,32,128]{3,2,0,1:T(8,128)S(1)}, f32[6,12,32,128]{3,2,0,1:T(8,128)S(1)}, u32[]{:S(2)}, u32[]{:S(2)}) %collective-permute-start.11) | collective-permute-done | bytes 1179680 | tf_op jit(solution)/shard_map/ppermute | solution.py:12
  310.0 3.3 collective-permute-start.12
  313.3 23.6 %collective-permute-done.12 = f32[12,12,16,128]{3,2,0,1:T(8,128)} collective-permute-done((f32[12,12,16,128]{3,2,0,1:T(8,128)S(1)}, f32[12,12,16,128]{3,2,0,1:T(8,128)}, u32[]{:S(2)}, u32[]{:S(2)}) %collective-permute-start.12) | collective-permute-done | bytes 1179680 | tf_op jit(solution)/shard_map/ppermute | solution.py:12
  338.4 2.5 constant_dynamic-slice_fusion
  341.6 3.1 collective-permute-start.14
  346.7 4.5 collective-permute-start.17
  354.8 64.8 %collective-permute-done.14 = f32[12,12,16,16]{3,2,0,1:T(8,128)S(1)} collective-permute-done((f32[12,12,16,16]{3,2,0,1:T(8,128)S(1)}, f32[12,12,16,16]{3,2,0,1:T(8,128)S(1)}, u32[]{:S(2)}, u32[]{:S(2)}) %collective-permute-start.14) | collective-permute-done | bytes 147488 | tf_op jit(solution)/shard_map/ppermute | solution.py:105
  419.6 2.5 collective-permute-start.19
  424.4 97.4 %collective-permute-done.16 = f32[12,12,16,16]{3,2,0,1:T(8,128)S(1)} collective-permute-done((f32[12,12,16,16]{3,2,0,1:T(8,128)S(1)}, f32[12,12,16,16]{3,2,0,1:T(8,128)S(1)}, u32[]{:S(2)}, u32[]{:S(2)}) %collective-permute-start.16) | collective-permute-done | bytes 147488 | tf_op jit(solution)/shard_map/ppermute | solution.py:105
  523.0 89.5 %collective-permute-done.17 = f32[12,12,16,16]{3,2,0,1:T(8,128)S(1)} collective-permute-done((f32[12,12,16,16]{3,2,0,1:T(8,128)S(1)}, f32[12,12,16,16]{3,2,0,1:T(8,128)S(1)}, u32[]{:S(2)}, u32[]{:S(2)}) %collective-permute-start.17) | collective-permute-done | bytes 147488 | tf_op jit(solution)/shard_map/ppermute | solution.py:105
  613.7 27.5 %collective-permute-done.18 = f32[12,12,16,16]{3,2,0,1:T(8,128)S(1)} collective-permute-done((f32[12,12,16,16]{3,2,0,1:T(8,128)S(1)}, f32[12,12,16,16]{3,2,0,1:T(8,128)S(1)}, u32[]{:S(2)}, u32[]{:S(2)}) %collective-permute-start.18) | collective-permute-done | bytes 147488 | tf_op jit(solution)/shard_map/ppermute | solution.py:105
  644.8 8.5 %gather_fusion.1 = f32[8,12,12,16,16]{4,3,1,2,0:T(8,128)} fusion(f32[8,12,12,16,16]{4,3,1,2,0:T(8,128)} %bitcast_dynamic-update-slice_fusion, s32[1024]{0:T(1024)S(1)} %pad_clamp_fusion), kind=kCustom, calls=%fused_computation.1 | custom fusion | bytes 2359328 | tf_op jit(solution)/shard_map/jit(_take)/gather | solution.py:108
  653.2 9.1 %select_bitcast_fusion = f32[12,12,16,8,16]{2,4,1,0,3:T(8,128)} fusion(f32[8,12,12,16,16]{4,3,1,2,0:T(8,128)} %gather_fusion.1, pred[8]{0:T(512)(128)(4,1)S(1)} %compare_and_fusion), kind=kLoop, calls=%fused_computation.7 | loop fusion | flops 294912 | bytes 2359304 | tf_op jit(solution)/shard_map/jit(_take)/select_n | solution.py:108
  662.3 9.7 %copy.31 = f32[12,12,16,8,16]{4,3,2,0,1:T(8,128)} copy(f32[12,12,16,8,16]{2,4,1,0,3:T(8,128)} %select_bitcast_fusion) | data formatting | bytes 2359296 | tf_op jit(solution)/shard_map/jit(_take)/select_n | solution.py:108
  672.0 6.2 reshape.218
  (74 shorter events, 59.1 us)
Async XLA Ops:
  18.0 2.4 copy-start.3
  20.0 53.1 %collective-permute-start = (bf16[12,60,12,128]{3,1,2,0:T(8,128)(2,1)S(1)}, bf16[12,60,12,128]{3,1,2,0:T(8,128)(2,1)S(1)}, u32[]{:S(2)}, u32[]{:S(2)}) collective-permute-start(bf16[12,60,12,128]{3,1,2,0:T(8,128)(2,1)S(1)} %broadcast_select_fusion.1), channel_id=1, source_target_pairs={{0,64},{32,96},{64,0},{96,32},{1,65},{33,97},{65,1},{97,33},{2,66}... | collective-permute-start | bytes 6635528 | tf_op jit(solution)/shard_map/ppermute | solution.py:12
  73.1 1.4 copy-start.1
  86.0 65.0 %collective-permute-start.1 = (bf16[2,12,60,12,128]{4,0,3,2,1:T(2,128)(2,1)}, bf16[2,12,60,12,128]{4,0,3,2,1:T(2,128)(2,1)}, u32[]{:S(2)}, u32[]{:S(2)}) collective-permute-start(bf16[2,12,60,12,128]{4,0,3,2,1:T(2,128)(2,1)} %copy.24), channel_id=1, source_target_pairs={{0,32},{32,0},{64,96},{96,64},{1,33},{33,1},{65,97},{97,65},{2,34}... | collective-permute-start | bytes 13271048 | tf_op jit(solution)/shard_map/ppermute | solution.py:12
  89.6 54.4 %collective-permute-start.3 = (bf16[12,12,60,128]{3,2,1,0:T(8,128)(2,1)}, bf16[12,12,60,128]{3,2,1,0:T(8,128)(2,1)}, u32[]{:S(2)}, u32[]{:S(2)}) collective-permute-start(bf16[12,12,60,128]{3,2,1,0:T(8,128)(2,1)} %broadcast_select_fusion), channel_id=1, source_target_pairs={{0,24},{8,16},{16,8},{24,0},{1,25},{9,17},{17,9},{25,1},{2,26},{10... | collective-permute-start | bytes 6635528 | tf_op jit(solution)/shard_map/ppermute | solution.py:12
  90.1 58.3 %collective-permute-start.2 = (bf16[12,12,60,128]{3,2,1,0:T(8,128)(2,1)}, bf16[12,12,60,128]{3,2,1,0:T(8,128)(2,1)}, u32[]{:S(2)}, u32[]{:S(2)}) collective-permute-start(bf16[12,12,60,128]{3,2,1,0:T(8,128)(2,1)} %broadcast_select_fusion), channel_id=1, source_target_pairs={{0,8},{8,0},{16,24},{24,16},{1,9},{9,1},{17,25},{25,17},{2,10},{10... | collective-permute-start | bytes 6635528 | tf_op jit(solution)/shard_map/ppermute | solution.py:12
  146.4 42.1 %collective-permute-start.4 = (bf16[6,12,60,128]{3,2,1,0:T(8,128)(2,1)}, bf16[6,12,60,128]{3,2,1,0:T(8,128)(2,1)}, u32[]{:S(2)}, u32[]{:S(2)}) collective-permute-start(bf16[6,12,60,128]{3,2,1,0:T(8,128)(2,1)} %slice.50), channel_id=1, source_target_pairs={{0,8},{8,0},{16,24},{24,16},{1,9},{9,1},{17,25},{25,17},{2,10},{10... | collective-permute-start | bytes 3317768 | tf_op jit(solution)/shard_map/ppermute | solution.py:12
  150.8 37.7 %collective-permute-start.5 = (bf16[6,12,60,128]{3,2,1,0:T(8,128)(2,1)}, bf16[6,12,60,128]{3,2,1,0:T(8,128)(2,1)}, u32[]{:S(2)}, u32[]{:S(2)}) collective-permute-start(bf16[6,12,60,128]{3,2,1,0:T(8,128)(2,1)} %slice.51), channel_id=1, source_target_pairs={{0,24},{8,16},{16,8},{24,0},{1,25},{9,17},{17,9},{25,1},{2,26},{10... | collective-permute-start | bytes 3317768 | tf_op jit(solution)/shard_map/ppermute | solution.py:12
  161.9 1.7 copy-start.2
  170.6 10.1 %copy-start.4 = (bf16[1,12,60,12,128]{4,2,3,1,0:T(8,128)(2,1)S(1)}, bf16[1,12,60,12,128]{4,2,3,1,0:T(8,128)(2,1)}, u32[]{:S(2)}) copy-start(bf16[1,12,60,12,128]{4,2,3,1,0:T(8,128)(2,1)} %get-tuple-element.9) | copy-start | bytes 6635524
  218.1 2.2 copy-start
  220.3 27.3 %collective-permute-start.9 = (f32[6,12,32,128]{3,2,0,1:T(8,128)S(1)}, f32[6,12,32,128]{3,2,0,1:T(8,128)S(1)}, u32[]{:S(2)}, u32[]{:S(2)}) collective-permute-start(f32[6,12,32,128]{3,2,0,1:T(8,128)S(1)} %constant_dynamic-slice_fusion.8), channel_id=1, source_target_pairs={{0,6},{1,7},{2,0},{3,1},{4,2},{5,3},{6,4},{7,5},{8,14},{9,15},{10,... | collective-permute-start | bytes 3538952 | tf_op jit(solution)/shard_map/ppermute | solution.py:12
  222.3 27.4 %collective-permute-start.6 = (f32[6,12,32,128]{3,2,0,1:T(8,128)S(1)}, f32[6,12,32,128]{3,2,0,1:T(8,128)}, u32[]{:S(2)}, u32[]{:S(2)}) collective-permute-start(f32[6,12,32,128]{3,2,0,1:T(8,128)S(1)} %constant_dynamic-slice_fusion.9), channel_id=1, source_target_pairs={{0,2},{1,3},{2,4},{3,5},{4,6},{5,7},{6,0},{7,1},{8,10},{9,11},{10,... | collective-permute-start | bytes 3538952 | tf_op jit(solution)/shard_map/ppermute | solution.py:12
  249.2 27.2 %collective-permute-start.10 = (f32[6,12,32,128]{3,2,0,1:T(8,128)S(1)}, f32[6,12,32,128]{3,2,0,1:T(8,128)S(1)}, u32[]{:S(2)}, u32[]{:S(2)}) collective-permute-start(f32[6,12,32,128]{3,2,0,1:T(8,128)S(1)} %dynamic-slice_add_fusion.2), channel_id=1, source_target_pairs={{0,6},{1,7},{2,0},{3,1},{4,2},{5,3},{6,4},{7,5},{8,14},{9,15},{10,... | collective-permute-start | bytes 3538952 | tf_op jit(solution)/shard_map/ppermute | solution.py:12
  251.6 26.4 %collective-permute-start.7 = (f32[6,12,32,128]{3,2,0,1:T(8,128)S(1)}, f32[6,12,32,128]{3,2,0,1:T(8,128)}, u32[]{:S(2)}, u32[]{:S(2)}) collective-permute-start(f32[6,12,32,128]{3,2,0,1:T(8,128)S(1)} %dynamic-slice_add_fusion.5), channel_id=1, source_target_pairs={{0,2},{1,3},{2,4},{3,5},{4,6},{5,7},{6,0},{7,1},{8,10},{9,11},{10,... | collective-permute-start | bytes 3538952 | tf_op jit(solution)/shard_map/ppermute | solution.py:12
  277.9 26.8 %collective-permute-start.11 = (f32[6,12,32,128]{3,2,0,1:T(8,128)S(1)}, f32[6,12,32,128]{3,2,0,1:T(8,128)S(1)}, u32[]{:S(2)}, u32[]{:S(2)}) collective-permute-start(f32[6,12,32,128]{3,2,0,1:T(8,128)S(1)} %dynamic-slice_add_fusion.1), channel_id=1, source_target_pairs={{0,6},{1,7},{2,0},{3,1},{4,2},{5,3},{6,4},{7,5},{8,14},{9,15},{10,... | collective-permute-start | bytes 3538952 | tf_op jit(solution)/shard_map/ppermute | solution.py:12
  280.9 26.9 %collective-permute-start.8 = (f32[6,12,32,128]{3,2,0,1:T(8,128)}, f32[6,12,32,128]{3,2,0,1:T(8,128)}, u32[]{:S(2)}, u32[]{:S(2)}) collective-permute-start(f32[6,12,32,128]{3,2,0,1:T(8,128)} %dynamic-slice_add_fusion.4), channel_id=1, source_target_pairs={{0,2},{1,3},{2,4},{3,5},{4,6},{5,7},{6,0},{7,1},{8,10},{9,11},{10,... | collective-permute-start | bytes 3538952 | tf_op jit(solution)/shard_map/ppermute | solution.py:12
  310.0 26.9 %collective-permute-start.12 = (f32[12,12,16,128]{3,2,0,1:T(8,128)S(1)}, f32[12,12,16,128]{3,2,0,1:T(8,128)}, u32[]{:S(2)}, u32[]{:S(2)}) collective-permute-start(f32[12,12,16,128]{3,2,0,1:T(8,128)S(1)} %fusion.17), channel_id=1, source_target_pairs={{0,1},{1,0},{2,3},{3,2},{4,5},{5,4},{6,7},{7,6},{8,9},{9,8},{10,11... | collective-permute-start | bytes 3538952 | tf_op jit(solution)/shard_map/ppermute | solution.py:12
  340.9 10.4 %collective-permute-start.13 = (f32[12,12,16,16]{3,2,0,1:T(8,128)S(1)}, f32[12,12,16,16]{3,2,0,1:T(8,128)S(1)}, u32[]{:S(2)}, u32[]{:S(2)}) collective-permute-start(f32[12,12,16,16]{3,2,0,1:T(8,128)S(1)} %get-tuple-element.20), channel_id=1, source_target_pairs={{0,0},{1,1},{2,2},{3,3},{4,4},{5,5},{6,6},{7,7},{8,32},{9,33},{10,... | collective-permute-start | bytes 442376 | tf_op jit(solution)/shard_map/ppermute | solution.py:105
  341.6 78.0 %collective-permute-start.14 = (f32[12,12,16,16]{3,2,0,1:T(8,128)S(1)}, f32[12,12,16,16]{3,2,0,1:T(8,128)S(1)}, u32[]{:S(2)}, u32[]{:S(2)}) collective-permute-start(f32[12,12,16,16]{3,2,0,1:T(8,128)S(1)} %get-tuple-element.19), channel_id=1, source_target_pairs={{0,1},{1,0},{2,3},{3,2},{4,5},{5,4},{6,7},{7,6},{8,33},{9,32},{10,... | collective-permute-start | bytes 442376 | tf_op jit(solution)/shard_map/ppermute | solution.py:105
  344.7 78.5 %collective-permute-start.15 = (f32[12,12,16,16]{3,2,0,1:T(8,128)S(1)}, f32[12,12,16,16]{3,2,0,1:T(8,128)S(1)}, u32[]{:S(2)}, u32[]{:S(2)}) collective-permute-start(f32[12,12,16,16]{3,2,0,1:T(8,128)S(1)} %get-tuple-element.18), channel_id=1, source_target_pairs={{0,2},{1,3},{2,0},{3,1},{4,6},{5,7},{6,4},{7,5},{8,34},{9,35},{10,... | collective-permute-start | bytes 442376 | tf_op jit(solution)/shard_map/ppermute | solution.py:105
  346.7 175.1 %collective-permute-start.16 = (f32[12,12,16,16]{3,2,0,1:T(8,128)S(1)}, f32[12,12,16,16]{3,2,0,1:T(8,128)S(1)}, u32[]{:S(2)}, u32[]{:S(2)}) collective-permute-start(f32[12,12,16,16]{3,2,0,1:T(8,128)S(1)} %get-tuple-element.17), channel_id=1, source_target_pairs={{0,3},{1,2},{2,1},{3,0},{4,7},{5,6},{6,5},{7,4},{8,35},{9,34},{10,... | collective-permute-start | bytes 442376 | tf_op jit(solution)/shard_map/ppermute | solution.py:105
  346.7 265.7 %collective-permute-start.17 = (f32[12,12,16,16]{3,2,0,1:T(8,128)S(1)}, f32[12,12,16,16]{3,2,0,1:T(8,128)S(1)}, u32[]{:S(2)}, u32[]{:S(2)}) collective-permute-start(f32[12,12,16,16]{3,2,0,1:T(8,128)S(1)} %get-tuple-element.16), channel_id=1, source_target_pairs={{0,4},{1,5},{2,6},{3,7},{4,0},{5,1},{6,2},{7,3},{8,36},{9,37},{10,... | collective-permute-start | bytes 442376 | tf_op jit(solution)/shard_map/ppermute | solution.py:105
  351.2 289.9 %collective-permute-start.18 = (f32[12,12,16,16]{3,2,0,1:T(8,128)S(1)}, f32[12,12,16,16]{3,2,0,1:T(8,128)S(1)}, u32[]{:S(2)}, u32[]{:S(2)}) collective-permute-start(f32[12,12,16,16]{3,2,0,1:T(8,128)S(1)} %get-tuple-element.15), channel_id=1, source_target_pairs={{0,5},{1,4},{2,7},{3,6},{4,1},{5,0},{6,3},{7,2},{8,37},{9,36},{10,... | collective-permute-start | bytes 442376 | tf_op jit(solution)/shard_map/ppermute | solution.py:105
  419.6 222.7 %collective-permute-start.19 = (f32[12,12,16,16]{3,2,0,1:T(8,128)S(1)}, f32[12,12,16,16]{3,2,0,1:T(8,128)S(1)}, u32[]{:S(2)}, u32[]{:S(2)}) collective-permute-start(f32[12,12,16,16]{3,2,0,1:T(8,128)S(1)} %get-tuple-element.14), channel_id=1, source_target_pairs={{0,6},{1,7},{2,4},{3,5},{4,2},{5,3},{6,0},{7,1},{8,38},{9,39},{10,... | collective-permute-start | bytes 442376 | tf_op jit(solution)/shard_map/ppermute | solution.py:105
  423.2 220.3 %collective-permute-start.20 = (f32[12,12,16,16]{3,2,0,1:T(8,128)S(1)}, f32[12,12,16,16]{3,2,0,1:T(8,128)S(1)}, u32[]{:S(2)}, u32[]{:S(2)}) collective-permute-start(f32[12,12,16,16]{3,2,0,1:T(8,128)S(1)} %get-tuple-element.13), channel_id=1, source_target_pairs={{0,7},{1,6},{2,5},{3,4},{4,3},{5,2},{6,1},{7,0},{8,39},{9,38},{10,... | collective-permute-start | bytes 442376 | tf_op jit(solution)/shard_map/ppermute | solution.py:105

commit v2 on v1

--- a/solution.py
+++ b/solution.py
@@ -76,6 +76,7 @@
 
     amp_x = gather_col(amp)
     int_x = gather_row(ints)
+    amp_x, int_x = lax.optimization_barrier((amp_x, int_x))
     part = None
     for v in range(4):
         u = (col_at ^ v) ^ row_at
@@ -92,21 +93,12 @@
 
     n_row = lax.axis_size("row")
     n_col = lax.axis_size("col")
-    axes = ("row", "col", "slab")
-    tiles = []
-    for d in range(n_slab):
-        dest_slab = slab_at ^ d
-        tile = lax.dynamic_slice_in_dim(shares, dest_slab * width, width, axis=3)
-        pairs = []
-        for r in range(n_row):
-            for c in range(n_col):
-                for t in range(n_slab):
-                    pairs.append(((r * n_col + c) * n_slab + t, (c * n_col + r) * n_slab + (t ^ d)))
-        tiles.append(lax.ppermute(tile, axes, pairs))
-    stacked = jnp.stack(tiles)
-    order = jnp.arange(n_slab, dtype=jnp.int32) ^ slab_at
-    ordered = jnp.take(stacked, order, axis=0)
-    mirrored = jnp.transpose(ordered, (2, 1, 4, 0, 3)).reshape(shares.shape)
+    i_n, j_n, a_n, b_n = shares.shape
+    tiles = jnp.transpose(shares.reshape(i_n, j_n, a_n, n_slab, b_n // n_slab), (3, 0, 1, 2, 4))
+    regrouped = lax.all_to_all(tiles, "slab", 0, 0, tiled=True)
+    pairs = [(r * n_col + c, c * n_col + r) for r in range(n_row) for c in range(n_col)]
+    swapped = lax.ppermute(regrouped, ("row", "col"), pairs)
+    mirrored = jnp.transpose(swapped, (2, 1, 4, 0, 3)).reshape(shares.shape)
     return (shares + mirrored).astype(jnp.bfloat16)
 
 

time: 683 us -> 660 us (0.966)
  the two profiles are of different devices: /device:TPU:52 before, /device:TPU:33 now
where the time goes in v2:
time: 660 us; the launch traced here: 652 us
  waiting for transfers between devices  422 us (64%)
  local copies, waits for them, and re-layouts  104 us (16%)
  other arithmetic  39.8 us (6%)
  matrix products  38.2 us (6%)
  starting transfers between devices  28.3 us (4%)
  blocking collectives  16.4 us (2%)
    ppermute x13, waiting for transfers between devices, shifted(): lax.ppermute(value, axis, [(src, fn(src) % size) for src in range(size)])  219 us
    ppermute x1, waiting for transfers between devices, body(): swapped = lax.ppermute(regrouped, ('row', 'col'), pairs)  203 us
    dot_general x4, matrix products, body(): jnp.einsum('ikca,kcjb->ijab', amp_x[v], int_blk, preferred_element_type=j...  38.2 us
    unnamed x27, local copies, waits for them, and re-layouts  30.6 us
    ppermute x13, starting transfers between devices, shifted(): lax.ppermute(value, axis, [(src, fn(src) % size) for src in range(size)])  18.9 us
    all_to_all x1, blocking collectives, body(): regrouped = lax.all_to_all(tiles, 'slab', 0, 0, tiled=True)  16.4 us
    reshape x2, local copies, waits for them, and re-layouts, body(): shares.reshape(i_n, j_n, a_n, n_slab, b_n // n_slab)  14.8 us
  transfers between devices with their start and end apart: 14, of which 12 were waited for; matrix products, arithmetic and copies ran while one was open for 3% of the time, Pallas kernels for 0%

profile of v2, /device:TPU:33, one launch (start us, length us, event | category | flops | bytes accessed | tf_op | source)
XLA Modules:
  0.0 651.6 jit_solution(8331041767601288825)
XLA Ops:
  6.1 11.9 %and_select_fusion.1 = s32[128]{0:T(128)S(1)} fusion(s32[]{:T(128)} %bitcast.27, s32[]{:T(128)} %bitcast.28, s32[]{:T(128)} %bitcast.29, s32[]{:T(128)} %bitcast.30, s32[]{:T(128)} %bitcast.31, s32[]{:T(128)} %bitcast.33, s32[]{:T(128)} %bitcast.32, s32[]{:T(128)} %bitcast.4, s32[]{:T(128)} %bitcast.6, s32[]{:T(128)} %bitcast.8, s32[]{:T(128)} %bitcast.10, ...), kind=kLoop, calls=%fused_computation.76 | loop fusion | flops 8192 | bytes 588 | tf_op jit(solution)/shard_map/jit(_take)/select_n | solution.py:19
  20.7 51.7 %collective-permute-done.4 = bf16[12,60,12,128]{3,1,2,0:T(8,128)(2,1)S(1)} collective-permute-done((bf16[12,60,12,128]{3,1,2,0:T(8,128)(2,1)S(1)}, bf16[12,60,12,128]{3,1,2,0:T(8,128)(2,1)S(1)}, u32[]{:S(2)}, u32[]{:S(2)}) %collective-permute-start.4) | collective-permute-done | bytes 2211872 | tf_op jit(solution)/shard_map/ppermute | solution.py:12
  76.4 9.0 %copy.25 = bf16[2,12,60,12,128]{4,0,3,2,1:T(2,128)(2,1)} copy(bf16[2,12,60,12,128]{4,2,3,1,0:T(8,128)(2,1)} %pad_maximum_fusion.1) | data formatting | bytes 8847360 | tf_op jit(solution)/shard_map/stack | solution.py:37
  93.2 51.5 %collective-permute-done.1 = bf16[12,12,60,128]{3,2,1,0:T(8,128)(2,1)S(1)} collective-permute-done((bf16[12,12,60,128]{3,2,1,0:T(8,128)(2,1)S(1)}, bf16[12,12,60,128]{3,2,1,0:T(8,128)(2,1)S(1)}, u32[]{:S(2)}, u32[]{:S(2)}) %collective-permute-start.1) | collective-permute-done | bytes 2211872 | tf_op jit(solution)/shard_map/ppermute | solution.py:12
  149.9 21.8 %collective-permute-done.2 = bf16[6,12,60,128]{3,2,1,0:T(8,128)(2,1)} collective-permute-done((bf16[6,12,60,128]{3,2,1,0:T(8,128)(2,1)S(1)}, bf16[6,12,60,128]{3,2,1,0:T(8,128)(2,1)}, u32[]{:S(2)}, u32[]{:S(2)}) %collective-permute-start.2) | collective-permute-done | bytes 1105952 | tf_op jit(solution)/shard_map/ppermute | solution.py:12
  171.7 4.9 collective-permute-done.3
  176.6 3.3 pad_maximum_fusion.2
  179.9 10.2 %fusion.25 = (bf16[1,12,60,12,128]{4,0,3,2,1:T(2,128)(2,1)S(1)}, bf16[1,12,60,12,128]{4,0,3,2,1:T(2,128)(2,1)S(1)}) fusion(bf16[2,12,60,12,128]{4,0,3,2,1:T(2,128)(2,1)} %collective-permute-done.5), kind=kLoop, calls=%fused_computation.97 | loop fusion | bytes 8847360 | tf_op jit(solution)/shard_map/slice | solution.py:39
  193.8 5.6 constant_dynamic-slice_fusion.2
  199.4 10.1 %fusion.6 = f32[12,128,12,128,1]{1,3,4,2,0:T(8,128)} fusion(bf16[12,12,60,128]{3,2,1,0:T(8,128)(2,1)} %copy-done.7, bf16[1,12,60,12,128]{4,2,3,1,0:T(8,128)(2,1)} %get-tuple-element.20), kind=kOutput, calls=%fused_computation.17 | convolution fusion | flops 3397386240 | bytes 13860864 | tf_op jit(solution)/shard_map/ikca,kcjb->ijab/dot_general | solution.py:84
  209.5 6.4 fusion.4
  215.9 6.5 %fusion.2 = f32[12,128,12,128,1]{1,3,4,2,0:T(8,128)} fusion(bf16[12,12,60,128]{3,2,1,0:T(8,128)(2,1)S(1)} %copy-done.8, bf16[1,12,60,12,128]{4,2,3,1,0:T(8,128)(2,1)S(1)} %copy-done.6), kind=kOutput, calls=%fused_computation.13 | convolution fusion | flops 3397386240 | bytes 13860864 | tf_op jit(solution)/shard_map/ikca,kcjb->ijab/dot_general | solution.py:84
  222.4 15.2 %fusion = f32[12,12,128,128]{3,2,0,1:T(8,128)} fusion(f32[12,128,12,128,1]{1,3,4,2,0:T(8,128)} %fusion.2, f32[12,128,12,128,1]{1,3,4,2,0:T(8,128)} %fusion.4, f32[12,128,12,128,1]{1,3,4,2,0:T(8,128)} %fusion.6, bf16[12,12,60,128]{3,2,1,0:T(8,128)(2,1)S(1)} %copy-done.5, bf16[1,12,60,12,128]{4,2,3,1,0:T(8,128)(2,1)S(1)} %get-tuple-element.17), kind=kOutput, calls=%fused_computation.3 | convolution fusion | flops 3404464128 | bytes 42172416 | tf_op jit(solution)/shard_map/ikca,kcjb->ijab/dot_general | solution.py:84
  237.6 6.9 %fusion.24 = (f32[6,12,128,128]{3,2,0,1:T(8,128)S(1)}, f32[6,12,128,128]{3,2,0,1:T(8,128)}) fusion(f32[12,12,128,128]{3,2,0,1:T(8,128)} %fusion), kind=kLoop, calls=%fused_computation.96 | loop fusion | bytes 18874368 | tf_op jit(solution)/shard_map/slice | solution.py:47
  251.2 22.1 %collective-permute-done.9 = f32[6,12,32,128]{3,2,0,1:T(8,128)S(1)} collective-permute-done((f32[6,12,32,128]{3,2,0,1:T(8,128)S(1)}, f32[6,12,32,128]{3,2,0,1:T(8,128)S(1)}, u32[]{:S(2)}, u32[]{:S(2)}) %collective-permute-start.9) | collective-permute-done | bytes 1179680 | tf_op jit(solution)/shard_map/ppermute | solution.py:12
  274.8 3.5 collective-permute-start.10
  280.3 20.7 %collective-permute-done.10 = f32[6,12,32,128]{3,2,0,1:T(8,128)S(1)} collective-permute-done((f32[6,12,32,128]{3,2,0,1:T(8,128)S(1)}, f32[6,12,32,128]{3,2,0,1:T(8,128)S(1)}, u32[]{:S(2)}, u32[]{:S(2)}) %collective-permute-start.10) | collective-permute-done | bytes 1179680 | tf_op jit(solution)/shard_map/ppermute | solution.py:12
  302.5 3.5 collective-permute-start.11
  309.2 18.7 %collective-permute-done.11 = f32[6,12,32,128]{3,2,0,1:T(8,128)S(1)} collective-permute-done((f32[6,12,32,128]{3,2,0,1:T(8,128)S(1)}, f32[6,12,32,128]{3,2,0,1:T(8,128)S(1)}, u32[]{:S(2)}, u32[]{:S(2)}) %collective-permute-start.11) | collective-permute-done | bytes 1179680 | tf_op jit(solution)/shard_map/ppermute | solution.py:12
  329.4 5.1 collective-permute-done.8
  339.4 21.9 %collective-permute-done.12 = f32[12,12,16,128]{3,2,0,1:T(8,128)} collective-permute-done((f32[12,12,16,128]{3,2,0,1:T(8,128)S(1)}, f32[12,12,16,128]{3,2,0,1:T(8,128)}, u32[]{:S(2)}, u32[]{:S(2)}) %collective-permute-start.12) | collective-permute-done | bytes 1179680 | tf_op jit(solution)/shard_map/ppermute | solution.py:12
  362.8 5.2 reshape.200
  368.0 9.6 %copy.32 = f32[12,12,16,8,16]{2,4,1,0,3:T(8,128)} copy(f32[12,12,16,8,16]{4,3,2,0,1:T(8,128)} %reshape.200) | data formatting | bytes 2359296 | tf_op jit(solution)/shard_map/reshape | solution.py:97
  377.6 8.5 %bitcast_bitcast_fusion = f32[8,12,12,16,16]{4,3,2,1,0:T(8,128)} fusion(f32[12,12,16,8,16]{2,4,1,0,3:T(8,128)} %copy.32), kind=kLoop, calls=%fused_computation.100 | loop fusion | bytes 2359296
  386.1 7.5 %reshape.299 = f32[8,1,36864]{2,1,0:T(1,128)S(1)} reshape(f32[8,12,12,16,16]{4,3,2,1,0:T(8,128)} %bitcast_bitcast_fusion) | data formatting | bytes 2359296
  393.7 16.4 %all_to_all.5 = f32[8,1,36864]{2,1,0:T(1,128)S(1)} all-to-all(f32[8,1,36864]{2,1,0:T(1,128)S(1)} %reshape.299), channel_id=1, replica_groups=mesh['row'=4,'col'=4,'slab'=8] {'slab'}, dimensions={0} | all-to-all | bytes 2359296 | tf_op jit(solution)/shard_map/all_to_all | solution.py:98
  410.6 3.4 reduce
  414.1 6.8 %reshape.300 = f32[8,12,12,16,16]{4,3,2,1,0:T(8,128)} reshape(f32[8,36864]{1,0:T(8,128)S(1)} %reduce) | data formatting | bytes 2359296
  420.9 9.4 %collective-permute-start.13 = (f32[8,12,12,16,16]{3,4,2,1,0:T(8,128)}, f32[8,12,12,16,16]{3,4,2,1,0:T(8,128)S(1)}, u32[]{:S(2)}, u32[]{:S(2)}) collective-permute-start(f32[8,12,12,16,16]{3,4,2,1,0:T(8,128)} %bitcast.174), channel_id=1, source_target_pairs={{0,0},{8,32},{16,64},{24,96},{32,8},{40,40},{48,72},{56,104},{64,1... | collective-permute-start | bytes 3538952 | tf_op jit(solution)/shard_map/ppermute | solution.py:100
  430.3 203.4 %collective-permute-done.13 = f32[8,12,12,16,16]{3,4,2,1,0:T(8,128)S(1)} collective-permute-done((f32[8,12,12,16,16]{3,4,2,1,0:T(8,128)}, f32[8,12,12,16,16]{3,4,2,1,0:T(8,128)S(1)}, u32[]{:S(2)}, u32[]{:S(2)}) %collective-permute-start.13) | collective-permute-done | bytes 1179680 | tf_op jit(solution)/shard_map/ppermute | solution.py:100
  633.7 10.2 %copy.33 = f32[12,12,16,8,16]{4,3,2,0,1:T(8,128)} copy(f32[12,12,16,8,16]{4,2,0,1,3:T(8,128)S(1)} %bitcast.175) | data formatting | bytes 2359296 | tf_op jit(solution)/shard_map/transpose | solution.py:101
  644.0 6.2 reshape.201
  (67 shorter events, 51.8 us)
Async XLA Ops:
  18.2 2.4 copy-start.3
  20.2 52.2 %collective-permute-start.4 = (bf16[12,60,12,128]{3,1,2,0:T(8,128)(2,1)S(1)}, bf16[12,60,12,128]{3,1,2,0:T(8,128)(2,1)S(1)}, u32[]{:S(2)}, u32[]{:S(2)}) collective-permute-start(bf16[12,60,12,128]{3,1,2,0:T(8,128)(2,1)S(1)} %broadcast_select_fusion), channel_id=1, source_target_pairs={{0,64},{32,96},{64,0},{96,32},{1,65},{33,97},{65,1},{97,33},{2,66}... | collective-permute-start | bytes 6635528 | tf_op jit(solution)/shard_map/ppermute | solution.py:12
  72.4 1.4 copy-start.1
  85.3 94.5 %collective-permute-start.5 = (bf16[2,12,60,12,128]{4,0,3,2,1:T(2,128)(2,1)}, bf16[2,12,60,12,128]{4,0,3,2,1:T(2,128)(2,1)}, u32[]{:S(2)}, u32[]{:S(2)}) collective-permute-start(bf16[2,12,60,12,128]{4,0,3,2,1:T(2,128)(2,1)} %copy.25), channel_id=1, source_target_pairs={{0,32},{32,0},{64,96},{96,64},{1,33},{33,1},{65,97},{97,65},{2,34}... | collective-permute-start | bytes 13271048 | tf_op jit(solution)/shard_map/ppermute | solution.py:12
  90.6 57.4 %copy-start.7 = (bf16[12,12,60,128]{3,2,1,0:T(8,128)(2,1)}, bf16[12,12,60,128]{3,2,1,0:T(8,128)(2,1)S(1)}, u32[]{:S(2)}) copy-start(bf16[12,12,60,128]{3,2,1,0:T(8,128)(2,1)S(1)} %broadcast_select_fusion.1) | copy-start | bytes 6635524
  90.6 54.1 %collective-permute-start.1 = (bf16[12,12,60,128]{3,2,1,0:T(8,128)(2,1)S(1)}, bf16[12,12,60,128]{3,2,1,0:T(8,128)(2,1)S(1)}, u32[]{:S(2)}, u32[]{:S(2)}) collective-permute-start(bf16[12,12,60,128]{3,2,1,0:T(8,128)(2,1)S(1)} %broadcast_select_fusion.1), channel_id=1, source_target_pairs={{0,24},{8,16},{16,8},{24,0},{1,25},{9,17},{17,9},{25,1},{2,26},{10... | collective-permute-start | bytes 6635528 | tf_op jit(solution)/shard_map/ppermute | solution.py:12
  93.2 52.1 %collective-permute-start = (bf16[12,12,60,128]{3,2,1,0:T(8,128)(2,1)S(1)}, bf16[12,12,60,128]{3,2,1,0:T(8,128)(2,1)S(1)}, u32[]{:S(2)}, u32[]{:S(2)}) collective-permute-start(bf16[12,12,60,128]{3,2,1,0:T(8,128)(2,1)S(1)} %broadcast_select_fusion.1), channel_id=1, source_target_pairs={{0,8},{8,0},{16,24},{24,16},{1,9},{9,1},{17,25},{25,17},{2,10},{10... | collective-permute-start | bytes 6635528 | tf_op jit(solution)/shard_map/ppermute | solution.py:12
  144.7 3.3 copy-start.4
  144.8 26.9 %collective-permute-start.2 = (bf16[6,12,60,128]{3,2,1,0:T(8,128)(2,1)S(1)}, bf16[6,12,60,128]{3,2,1,0:T(8,128)(2,1)}, u32[]{:S(2)}, u32[]{:S(2)}) collective-permute-start(bf16[6,12,60,128]{3,2,1,0:T(8,128)(2,1)S(1)} %slice.46), channel_id=1, source_target_pairs={{0,8},{8,0},{16,24},{24,16},{1,9},{9,1},{17,25},{25,17},{2,10},{10... | collective-permute-start | bytes 3317768 | tf_op jit(solution)/shard_map/ppermute | solution.py:12
  145.2 1.6 copy-start.9
  148.0 28.6 %collective-permute-start.3 = (bf16[6,12,60,128]{3,2,1,0:T(8,128)(2,1)}, bf16[6,12,60,128]{3,2,1,0:T(8,128)(2,1)}, u32[]{:S(2)}, u32[]{:S(2)}) collective-permute-start(bf16[6,12,60,128]{3,2,1,0:T(8,128)(2,1)} %slice.47), channel_id=1, source_target_pairs={{0,24},{8,16},{16,8},{24,0},{1,25},{9,17},{17,9},{25,1},{2,26},{10... | collective-permute-start | bytes 3317768 | tf_op jit(solution)/shard_map/ppermute | solution.py:12
  190.8 1.7 copy-start.2
  199.4 10.1 %copy-start.10 = (bf16[12,12,60,128]{3,2,1,0:T(8,128)(2,1)S(1)}, bf16[12,12,60,128]{3,2,1,0:T(8,128)(2,1)}, u32[]{:S(2)}) copy-start(bf16[12,12,60,128]{3,2,1,0:T(8,128)(2,1)} %copy-done.9) | copy-start | bytes 6635524
  209.5 6.4 copy-start.6
  209.5 6.4 copy-start.8
  215.9 6.5 %copy-start.5 = (bf16[12,12,60,128]{3,2,1,0:T(8,128)(2,1)S(1)}, bf16[12,12,60,128]{3,2,1,0:T(8,128)(2,1)}, u32[]{:S(2)}) copy-start(bf16[12,12,60,128]{3,2,1,0:T(8,128)(2,1)} %copy-done.4) | copy-start | bytes 6635524
  244.6 2.2 copy-start
  246.8 26.4 %collective-permute-start.9 = (f32[6,12,32,128]{3,2,0,1:T(8,128)S(1)}, f32[6,12,32,128]{3,2,0,1:T(8,128)S(1)}, u32[]{:S(2)}, u32[]{:S(2)}) collective-permute-start(f32[6,12,32,128]{3,2,0,1:T(8,128)S(1)} %constant_dynamic-slice_fusion), channel_id=1, source_target_pairs={{0,6},{1,7},{2,0},{3,1},{4,2},{5,3},{6,4},{7,5},{8,14},{9,15},{10,... | collective-permute-start | bytes 3538952 | tf_op jit(solution)/shard_map/ppermute | solution.py:12
  251.1 27.2 %collective-permute-start.6 = (f32[6,12,32,128]{3,2,0,1:T(8,128)S(1)}, f32[6,12,32,128]{3,2,0,1:T(8,128)}, u32[]{:S(2)}, u32[]{:S(2)}) collective-permute-start(f32[6,12,32,128]{3,2,0,1:T(8,128)S(1)} %constant_dynamic-slice_fusion.1), channel_id=1, source_target_pairs={{0,2},{1,3},{2,4},{3,5},{4,6},{5,7},{6,0},{7,1},{8,10},{9,11},{10,... | collective-permute-start | bytes 3538952 | tf_op jit(solution)/shard_map/ppermute | solution.py:12
  274.8 26.2 %collective-permute-start.10 = (f32[6,12,32,128]{3,2,0,1:T(8,128)S(1)}, f32[6,12,32,128]{3,2,0,1:T(8,128)S(1)}, u32[]{:S(2)}, u32[]{:S(2)}) collective-permute-start(f32[6,12,32,128]{3,2,0,1:T(8,128)S(1)} %dynamic-slice_add_fusion.2), channel_id=1, source_target_pairs={{0,6},{1,7},{2,0},{3,1},{4,2},{5,3},{6,4},{7,5},{8,14},{9,15},{10,... | collective-permute-start | bytes 3538952 | tf_op jit(solution)/shard_map/ppermute | solution.py:12
  280.2 26.1 %collective-permute-start.7 = (f32[6,12,32,128]{3,2,0,1:T(8,128)S(1)}, f32[6,12,32,128]{3,2,0,1:T(8,128)}, u32[]{:S(2)}, u32[]{:S(2)}) collective-permute-start(f32[6,12,32,128]{3,2,0,1:T(8,128)S(1)} %dynamic-slice_add_fusion.5), channel_id=1, source_target_pairs={{0,2},{1,3},{2,4},{3,5},{4,6},{5,7},{6,0},{7,1},{8,10},{9,11},{10,... | collective-permute-start | bytes 3538952 | tf_op jit(solution)/shard_map/ppermute | solution.py:12
  302.5 25.4 %collective-permute-start.11 = (f32[6,12,32,128]{3,2,0,1:T(8,128)S(1)}, f32[6,12,32,128]{3,2,0,1:T(8,128)S(1)}, u32[]{:S(2)}, u32[]{:S(2)}) collective-permute-start(f32[6,12,32,128]{3,2,0,1:T(8,128)S(1)} %dynamic-slice_add_fusion.1), channel_id=1, source_target_pairs={{0,6},{1,7},{2,0},{3,1},{4,2},{5,3},{6,4},{7,5},{8,14},{9,15},{10,... | collective-permute-start | bytes 3538952 | tf_op jit(solution)/shard_map/ppermute | solution.py:12
  309.2 25.3 %collective-permute-start.8 = (f32[6,12,32,128]{3,2,0,1:T(8,128)}, f32[6,12,32,128]{3,2,0,1:T(8,128)}, u32[]{:S(2)}, u32[]{:S(2)}) collective-permute-start(f32[6,12,32,128]{3,2,0,1:T(8,128)} %dynamic-slice_add_fusion.4), channel_id=1, source_target_pairs={{0,2},{1,3},{2,4},{3,5},{4,6},{5,7},{6,0},{7,1},{8,10},{9,11},{10,... | collective-permute-start | bytes 3538952 | tf_op jit(solution)/shard_map/ppermute | solution.py:12
  336.6 24.7 %collective-permute-start.12 = (f32[12,12,16,128]{3,2,0,1:T(8,128)S(1)}, f32[12,12,16,128]{3,2,0,1:T(8,128)}, u32[]{:S(2)}, u32[]{:S(2)}) collective-permute-start(f32[12,12,16,128]{3,2,0,1:T(8,128)S(1)} %fusion.16), channel_id=1, source_target_pairs={{0,1},{1,0},{2,3},{3,2},{4,5},{5,4},{6,7},{7,6},{8,9},{9,8},{10,11... | collective-permute-start | bytes 3538952 | tf_op jit(solution)/shard_map/ppermute | solution.py:12
  420.9 212.9 %collective-permute-start.13 = (f32[8,12,12,16,16]{3,4,2,1,0:T(8,128)}, f32[8,12,12,16,16]{3,4,2,1,0:T(8,128)S(1)}, u32[]{:S(2)}, u32[]{:S(2)}) collective-permute-start(f32[8,12,12,16,16]{3,4,2,1,0:T(8,128)} %bitcast.174), channel_id=1, source_target_pairs={{0,0},{8,32},{16,64},{24,96},{32,8},{40,40},{48,72},{56,104},{64,1... | collective-permute-start | bytes 3538952 | tf_op jit(solution)/shard_map/ppermute | solution.py:100

commit v3 on v2

--- a/solution.py
+++ b/solution.py
@@ -20,16 +20,6 @@
     occ = irreps[row_at] + irreps[col_at]
     parity = occ + label_c[:, None] + label_b[None, :]
     return parity % 2 == 0
-
-
-def gather_col(amp):
-    near1 = shifted(amp, "col", lambda c: c ^ 1)
-    near3 = shifted(amp, "col", lambda c: c ^ 3)
-    half = amp.shape[0] // 2
-    far_a = shifted(near3[:half], "col", lambda c: c ^ 1)
-    far_b = shifted(near1[half:], "col", lambda c: c ^ 3)
-    far = jnp.concatenate([far_a, far_b], axis=0)
-    return [amp, near1, far, near3]
 
 
 def gather_row(ints):
@@ -74,15 +64,11 @@
     mask = int_mask(irreps, blocks, row_at, col_at, slab_at, c_cols, win_cols)
     ints = jnp.where(mask[None, :, None, :], integrals, jnp.zeros_like(integrals))
 
-    amp_x = gather_col(amp)
+    amp_all = lax.all_gather(amp, "col", axis=1, tiled=True)
     int_x = gather_row(ints)
-    amp_x, int_x = lax.optimization_barrier((amp_x, int_x))
-    part = None
-    for v in range(4):
-        u = (col_at ^ v) ^ row_at
-        int_blk = lax.dynamic_index_in_dim(int_x, u, axis=0, keepdims=False)
-        term = jnp.einsum("ikca,kcjb->ijab", amp_x[v], int_blk, preferred_element_type=jnp.float32)
-        part = term if part is None else part + term
+    order = jnp.arange(int_x.shape[0], dtype=jnp.int32) ^ row_at
+    int_abs = jnp.take(int_x, order, axis=0).reshape(amp_all.shape[1], c_cols, -1, win_cols)
+    part = jnp.einsum("ikca,kcjb->ijab", amp_all, int_abs, preferred_element_type=jnp.float32)
 
     reduced_y = ring_reduce_y(part, slab_at)
     zh = slab_at % 2
@@ -91,14 +77,12 @@
     theirs = lax.dynamic_slice_in_dim(reduced_y, (1 - zh) * width, width, axis=2)
     shares = mine + shifted(theirs, "slab", lambda s: s ^ 1)
 
-    n_row = lax.axis_size("row")
-    n_col = lax.axis_size("col")
-    i_n, j_n, a_n, b_n = shares.shape
-    tiles = jnp.transpose(shares.reshape(i_n, j_n, a_n, n_slab, b_n // n_slab), (3, 0, 1, 2, 4))
-    regrouped = lax.all_to_all(tiles, "slab", 0, 0, tiled=True)
-    pairs = [(r * n_col + c, c * n_col + r) for r in range(n_row) for c in range(n_col)]
-    swapped = lax.ppermute(regrouped, ("row", "col"), pairs)
-    mirrored = jnp.transpose(swapped, (2, 1, 4, 0, 3)).reshape(shares.shape)
+    spread = lax.all_to_all(shares, "slab", 3, 2, tiled=True)
+    mirrored = jnp.transpose(spread, (1, 0, 3, 2))
+    for bit_no in range(lax.axis_size("row").bit_length() - 1):
+        across = shifted(shifted(mirrored, "row", lambda r: r ^ 2**bit_no), "col", lambda c: c ^ 2**bit_no)
+        differ = row_at // 2**bit_no % 2 != col_at // 2**bit_no % 2
+        mirrored = jnp.where(differ, across, mirrored)
     return (shares + mirrored).astype(jnp.bfloat16)
 
 

time: 660 us -> 477 us (0.72)
  the two profiles are of different devices: /device:TPU:33 before, /device:TPU:0 now
where the time goes in v3:
time: 477 us; the launch traced here: 470 us
  waiting for transfers between devices  237 us (50%)
  local copies, waits for them, and re-layouts  114 us (24%)
  other arithmetic  38.9 us (8%)
  starting transfers between devices  23.6 us (5%)
  matrix products  21.2 us (4%)
  blocking collectives  19.4 us (4%)
  between operations  16.2 us (3%)
    ppermute x13, waiting for transfers between devices, shifted(): lax.ppermute(value, axis, [(src, fn(src) % size) for src in range(size)])  237 us
    gather x12, local copies, waits for them, and re-layouts  29.1 us
    unnamed x16, local copies, waits for them, and re-layouts  25.4 us
    ppermute x13, starting transfers between devices, shifted(): lax.ppermute(value, axis, [(src, fn(src) % size) for src in range(size)])  23.6 us
    dot_general x1, matrix products, body(): jnp.einsum('ikca,kcjb->ijab', amp_all, int_abs, preferred_element_type=jn...  21.2 us
    all_to_all x3, local copies, waits for them, and re-layouts, body(): spread = lax.all_to_all(shares, 'slab', 3, 2, tiled=True)  20.7 us
    all_to_all x1, blocking collectives, body(): spread = lax.all_to_all(shares, 'slab', 3, 2, tiled=True)  19.4 us
    select_n x1, other arithmetic, int_mask(): label_b = jnp.take(irreps, blocks + b_ids // VTILE)  11.5 us
  transfers between devices with their start and end apart: 14, of which 12 were waited for; matrix products, arithmetic and copies ran while one was open for 17% of the time, Pallas kernels for 0%

profile of v3, /device:TPU:0, one launch (start us, length us, event | category | flops | bytes accessed | tf_op | source)
XLA Modules:
  0.0 470.5 jit_solution(2495726135807237858)
XLA Ops:
  8.5 3.3 broadcast_select_fusion
  15.7 11.5 %and_select_fusion.1 = s32[128]{0:T(128)S(1)} fusion(s32[]{:T(128)} %bitcast.26, s32[]{:T(128)} %bitcast.27, s32[]{:T(128)} %bitcast.28, s32[]{:T(128)} %bitcast.29, s32[]{:T(128)} %bitcast.30, s32[]{:T(128)} %bitcast.32, s32[]{:T(128)} %bitcast.31, s32[]{:T(128)} %bitcast.3, s32[]{:T(128)} %bitcast.5, s32[]{:T(128)} %bitcast.7, s32[]{:T(128)} %bitcast.9, ...), kind=kLoop, calls=%fused_computation.66 | loop fusion | flops 8192 | bytes 588 | tf_op jit(solution)/shard_map/jit(_take)/select_n | solution.py:19
  29.8 50.1 %collective-permute-done = bf16[12,60,12,128]{3,1,2,0:T(8,128)(2,1)S(1)} collective-permute-done((bf16[12,60,12,128]{3,1,2,0:T(8,128)(2,1)S(1)}, bf16[12,60,12,128]{3,1,2,0:T(8,128)(2,1)S(1)}, u32[]{:S(2)}, u32[]{:S(2)}) %collective-permute-start) | collective-permute-done | bytes 2211872 | tf_op jit(solution)/shard_map/ppermute | solution.py:12
  83.9 9.1 %copy.13 = bf16[2,12,60,12,128]{4,0,3,2,1:T(2,128)(2,1)} copy(bf16[2,12,60,12,128]{4,2,3,1,0:T(8,128)(2,1)} %pad_maximum_fusion.1) | data formatting | bytes 8847360 | tf_op jit(solution)/shard_map/stack | solution.py:27
  93.4 7.6 %collective-permute-done.1 = bf16[2,12,60,12,128]{4,0,3,2,1:T(2,128)(2,1)} collective-permute-done((bf16[2,12,60,12,128]{4,0,3,2,1:T(2,128)(2,1)}, bf16[2,12,60,12,128]{4,0,3,2,1:T(2,128)(2,1)}, u32[]{:S(2)}, u32[]{:S(2)}) %collective-permute-start.1) | collective-permute-done | bytes 4423712 | tf_op jit(solution)/shard_map/ppermute | solution.py:12
  101.0 10.2 %fusion.20 = (bf16[1,12,60,12,128]{4,0,3,2,1:T(2,128)(2,1)S(1)}, bf16[1,12,60,12,128]{4,0,3,2,1:T(2,128)(2,1)S(1)}) fusion(bf16[2,12,60,12,128]{4,0,3,2,1:T(2,128)(2,1)} %collective-permute-done.1), kind=kLoop, calls=%fused_computation.89 | loop fusion | bytes 8847360 | tf_op jit(solution)/shard_map/slice | solution.py:29
  113.6 4.3 pad_maximum_fusion
  117.8 29.1 %while.1 = (s32[]{:T(128)}, bf16[4,12,60,12,128]{4,2,3,1,0:T(8,128)(2,1)}, s32[4,1]{0,1:T(1,128)S(1)}, bf16[4,12,60,12,128]{4,3,2,1,0:T(8,128)(2,1)}, s32[]{:T(128)}) while((s32[]{:T(128)}, bf16[4,12,60,12,128]{4,2,3,1,0:T(8,128)(2,1)}, s32[4,1]{0,1:T(1,128)S(1)}, bf16[4,12,60,12,128]{4,3,2,1,0:T(8,128)(2,1)}, s32[]{:T(128)}) %tuple.38), condition=%wide.while_cond, body=%wide.while_body.sunk | while | flops 2 | bytes 9585229 | solution.py:70
  121.8 3.4 copy_dynamic-update-slice_fusion.2
  129.1 3.4 copy_dynamic-update-slice_fusion.2
  136.3 3.3 copy_dynamic-update-slice_fusion.2
  143.6 3.4 copy_dynamic-update-slice_fusion.2
  146.9 21.2 %fusion.5 = f32[12,12,128,128]{3,2,0,1:T(8,128)S(1)} fusion(bf16[12,48,60,128]{3,2,1,0:T(8,128)(2,1)} %all-gather.2.cloned.1.call-done, bf16[48,60,12,128]{3,2,1,0:T(8,128)(2,1)} %bitcast.141, pred[48]{0:T(512)(128)(4,1)S(1)} %broadcast_in_dim.44), kind=kOutput, calls=%fused_computation.13 | convolution fusion | flops 13593968640 | bytes 27131952 | tf_op jit(solution)/shard_map/ikca,kcjb->ijab/dot_general | solution.py:71
  173.5 3.9 collective-permute-start.5
  179.2 23.8 %collective-permute-done.5 = f32[6,12,32,128]{3,2,0,1:T(8,128)S(1)} collective-permute-done((f32[6,12,32,128]{3,2,0,1:T(8,128)S(1)}, f32[6,12,32,128]{3,2,0,1:T(8,128)S(1)}, u32[]{:S(2)}, u32[]{:S(2)}) %collective-permute-start.5) | collective-permute-done | bytes 1179680 | tf_op jit(solution)/shard_map/ppermute | solution.py:12
  204.4 3.8 collective-permute-start.6
  210.3 22.6 %collective-permute-done.6 = f32[6,12,32,128]{3,2,0,1:T(8,128)S(1)} collective-permute-done((f32[6,12,32,128]{3,2,0,1:T(8,128)S(1)}, f32[6,12,32,128]{3,2,0,1:T(8,128)S(1)}, u32[]{:S(2)}, u32[]{:S(2)}) %collective-permute-start.6) | collective-permute-done | bytes 1179680 | tf_op jit(solution)/shard_map/ppermute | solution.py:12
  234.4 3.8 collective-permute-start.7
  241.4 20.6 %collective-permute-done.7 = f32[6,12,32,128]{3,2,0,1:T(8,128)S(1)} collective-permute-done((f32[6,12,32,128]{3,2,0,1:T(8,128)S(1)}, f32[6,12,32,128]{3,2,0,1:T(8,128)S(1)}, u32[]{:S(2)}, u32[]{:S(2)}) %collective-permute-start.7) | collective-permute-done | bytes 1179680 | tf_op jit(solution)/shard_map/ppermute | solution.py:12
  263.5 5.4 %collective-permute-done.4 = f32[6,12,32,128]{3,2,0,1:T(8,128)} collective-permute-done((f32[6,12,32,128]{3,2,0,1:T(8,128)}, f32[6,12,32,128]{3,2,0,1:T(8,128)}, u32[]{:S(2)}, u32[]{:S(2)}) %collective-permute-start.4) | collective-permute-done | bytes 1179680 | tf_op jit(solution)/shard_map/ppermute | solution.py:12
  271.0 3.9 collective-permute-start.8
  274.9 23.5 %collective-permute-done.8 = f32[12,12,16,128]{3,2,0,1:T(8,128)} collective-permute-done((f32[12,12,16,128]{3,2,0,1:T(8,128)S(1)}, f32[12,12,16,128]{3,2,0,1:T(8,128)}, u32[]{:S(2)}, u32[]{:S(2)}) %collective-permute-start.8) | collective-permute-done | bytes 1179680 | tf_op jit(solution)/shard_map/ppermute | solution.py:12
  300.0 10.5 %copy.18 = f32[12,12,16,128]{2,0,1,3:T(8,128)} copy(f32[12,12,16,128]{3,2,0,1:T(8,128)S(1)} %fusion.12) | data formatting | bytes 2359296 | tf_op jit(solution)/shard_map/add | solution.py:78
  310.4 8.8 %reshape.328 = f32[8,1,36864]{2,1,0:T(1,128)S(1)} reshape(f32[128,12,12,16]{3,2,1,0:T(8,128)} %bitcast.135) | data formatting | bytes 2359296
  319.3 19.4 %all_to_all.18 = f32[8,1,36864]{2,1,0:T(1,128)S(1)} all-to-all(f32[8,1,36864]{2,1,0:T(1,128)S(1)} %reshape.328), channel_id=1, replica_groups=mesh['row'=4,'col'=4,'slab'=8] {'slab'}, dimensions={0} | all-to-all | bytes 2359296 | tf_op jit(solution)/shard_map/all_to_all | solution.py:80
  339.2 3.4 reduce
  342.6 10.0 %reshape.329 = f32[128,12,12,16]{3,2,1,0:T(8,128)} reshape(f32[8,36864]{1,0:T(8,128)S(1)} %reduce) | data formatting | bytes 2359296
  352.7 13.9 %copy.34 = f32[12,12,16,8,16]{2,3,4,1,0:T(8,128)} copy(f32[12,12,16,8,16]{2,0,1,4,3:T(8,128)} %bitcast.136) | data formatting | bytes 2359296 | tf_op jit(solution)/shard_map/all_to_all | solution.py:80
  366.6 6.2 %all_to_all.16 = f32[12,12,128,16]{2,3,1,0:T(8,128)S(1)} reshape(f32[12,12,8,16,16]{3,2,4,1,0:T(8,128)} %bitcast.137) | data formatting | bytes 2359296 | tf_op jit(solution)/shard_map/all_to_all | solution.py:80
  377.1 26.7 %collective-permute-done.10 = f32[12,12,16,128]{3,2,0,1:T(8,128)} collective-permute-done((f32[12,12,16,128]{3,2,0,1:T(8,128)S(1)}, f32[12,12,16,128]{3,2,0,1:T(8,128)}, u32[]{:S(2)}, u32[]{:S(2)}) %collective-permute-start.10) | collective-permute-done | bytes 1179680 | tf_op jit(solution)/shard_map/ppermute | solution.py:12
  405.5 27.2 %collective-permute-done.11 = f32[12,12,16,128]{3,2,0,1:T(8,128)} collective-permute-done((f32[12,12,16,128]{3,2,0,1:T(8,128)S(1)}, f32[12,12,16,128]{3,2,0,1:T(8,128)}, u32[]{:S(2)}, u32[]{:S(2)}) %collective-permute-start.11) | collective-permute-done | bytes 1179680 | tf_op jit(solution)/shard_map/ppermute | solution.py:12
  435.4 26.5 %collective-permute-done.12 = f32[12,12,16,128]{3,2,0,1:T(8,128)S(1)} collective-permute-done((f32[12,12,16,128]{3,2,0,1:T(8,128)}, f32[12,12,16,128]{3,2,0,1:T(8,128)S(1)}, u32[]{:S(2)}, u32[]{:S(2)}) %collective-permute-start.12) | collective-permute-done | bytes 1179680 | tf_op jit(solution)/shard_map/ppermute | solution.py:12
  (68 shorter events, 59.6 us)
Async XLA Ops:
  6.5 140.4 %all-gather.2.cloned.1.call-start = ((), (), s32[]{:S(2)}) async-start(), calls=%async_computation.1 | async-start | bytes 11796480 | tf_op jit(solution)/shard_map/all_gather | solution.py:67
  11.7 0.7 copy-start
  11.7 15.6 %copy-start.4 = (bf16[12,60,12,128]{3,1,2,0:T(8,128)(2,1)S(1)}, bf16[12,60,12,128]{3,1,2,0:T(8,128)(2,1)}, u32[]{:S(2)}) copy-start(bf16[12,60,12,128]{3,1,2,0:T(8,128)(2,1)} %param.5) | copy-start | bytes 6635524
  27.4 2.3 copy-start.5
  27.5 52.4 %collective-permute-start = (bf16[12,60,12,128]{3,1,2,0:T(8,128)(2,1)S(1)}, bf16[12,60,12,128]{3,1,2,0:T(8,128)(2,1)S(1)}, u32[]{:S(2)}, u32[]{:S(2)}) collective-permute-start(bf16[12,60,12,128]{3,1,2,0:T(8,128)(2,1)S(1)} %broadcast_select_fusion.1), channel_id=1, source_target_pairs={{0,64},{32,96},{64,0},{96,32},{1,65},{33,97},{65,1},{97,33},{2,66}... | collective-permute-start | bytes 6635528 | tf_op jit(solution)/shard_map/ppermute | solution.py:12
  79.9 1.5 copy-start.2
  93.0 8.0 %collective-permute-start.1 = (bf16[2,12,60,12,128]{4,0,3,2,1:T(2,128)(2,1)}, bf16[2,12,60,12,128]{4,0,3,2,1:T(2,128)(2,1)}, u32[]{:S(2)}, u32[]{:S(2)}) collective-permute-start(bf16[2,12,60,12,128]{4,0,3,2,1:T(2,128)(2,1)} %copy.13), channel_id=1, source_target_pairs={{0,32},{32,0},{64,96},{96,64},{1,33},{33,1},{65,97},{97,65},{2,34}... | collective-permute-start | bytes 13271048 | tf_op jit(solution)/shard_map/ppermute | solution.py:12
  111.9 1.7 copy-start.3
  171.3 2.2 copy-start.1
  173.5 29.4 %collective-permute-start.5 = (f32[6,12,32,128]{3,2,0,1:T(8,128)S(1)}, f32[6,12,32,128]{3,2,0,1:T(8,128)S(1)}, u32[]{:S(2)}, u32[]{:S(2)}) collective-permute-start(f32[6,12,32,128]{3,2,0,1:T(8,128)S(1)} %constant_dynamic-slice_fusion.2), channel_id=1, source_target_pairs={{0,6},{1,7},{2,0},{3,1},{4,2},{5,3},{6,4},{7,5},{8,14},{9,15},{10,... | collective-permute-start | bytes 3538952 | tf_op jit(solution)/shard_map/ppermute | solution.py:12
  178.8 29.4 %collective-permute-start.2 = (f32[6,12,32,128]{3,2,0,1:T(8,128)S(1)}, f32[6,12,32,128]{3,2,0,1:T(8,128)}, u32[]{:S(2)}, u32[]{:S(2)}) collective-permute-start(f32[6,12,32,128]{3,2,0,1:T(8,128)S(1)} %constant_dynamic-slice_fusion.3), channel_id=1, source_target_pairs={{0,2},{1,3},{2,4},{3,5},{4,6},{5,7},{6,0},{7,1},{8,10},{9,11},{10,... | collective-permute-start | bytes 3538952 | tf_op jit(solution)/shard_map/ppermute | solution.py:12
  204.4 28.4 %collective-permute-start.6 = (f32[6,12,32,128]{3,2,0,1:T(8,128)S(1)}, f32[6,12,32,128]{3,2,0,1:T(8,128)S(1)}, u32[]{:S(2)}, u32[]{:S(2)}) collective-permute-start(f32[6,12,32,128]{3,2,0,1:T(8,128)S(1)} %dynamic-slice_add_fusion.2), channel_id=1, source_target_pairs={{0,6},{1,7},{2,0},{3,1},{4,2},{5,3},{6,4},{7,5},{8,14},{9,15},{10,... | collective-permute-start | bytes 3538952 | tf_op jit(solution)/shard_map/ppermute | solution.py:12
  210.2 28.3 %collective-permute-start.3 = (f32[6,12,32,128]{3,2,0,1:T(8,128)S(1)}, f32[6,12,32,128]{3,2,0,1:T(8,128)}, u32[]{:S(2)}, u32[]{:S(2)}) collective-permute-start(f32[6,12,32,128]{3,2,0,1:T(8,128)S(1)} %dynamic-slice_add_fusion.5), channel_id=1, source_target_pairs={{0,2},{1,3},{2,4},{3,5},{4,6},{5,7},{6,0},{7,1},{8,10},{9,11},{10,... | collective-permute-start | bytes 3538952 | tf_op jit(solution)/shard_map/ppermute | solution.py:12
  234.4 27.6 %collective-permute-start.7 = (f32[6,12,32,128]{3,2,0,1:T(8,128)S(1)}, f32[6,12,32,128]{3,2,0,1:T(8,128)S(1)}, u32[]{:S(2)}, u32[]{:S(2)}) collective-permute-start(f32[6,12,32,128]{3,2,0,1:T(8,128)S(1)} %dynamic-slice_add_fusion.1), channel_id=1, source_target_pairs={{0,6},{1,7},{2,0},{3,1},{4,2},{5,3},{6,4},{7,5},{8,14},{9,15},{10,... | collective-permute-start | bytes 3538952 | tf_op jit(solution)/shard_map/ppermute | solution.py:12
  241.4 27.5 %collective-permute-start.4 = (f32[6,12,32,128]{3,2,0,1:T(8,128)}, f32[6,12,32,128]{3,2,0,1:T(8,128)}, u32[]{:S(2)}, u32[]{:S(2)}) collective-permute-start(f32[6,12,32,128]{3,2,0,1:T(8,128)} %dynamic-slice_add_fusion.4), channel_id=1, source_target_pairs={{0,2},{1,3},{2,4},{3,5},{4,6},{5,7},{6,0},{7,1},{8,10},{9,11},{10,... | collective-permute-start | bytes 3538952 | tf_op jit(solution)/shard_map/ppermute | solution.py:12
  271.0 27.5 %collective-permute-start.8 = (f32[12,12,16,128]{3,2,0,1:T(8,128)S(1)}, f32[12,12,16,128]{3,2,0,1:T(8,128)}, u32[]{:S(2)}, u32[]{:S(2)}) collective-permute-start(f32[12,12,16,128]{3,2,0,1:T(8,128)S(1)} %fusion.10), channel_id=1, source_target_pairs={{0,1},{1,0},{2,3},{3,2},{4,5},{5,4},{6,7},{7,6},{8,9},{9,8},{10,11... | collective-permute-start | bytes 3538952 | tf_op jit(solution)/shard_map/ppermute | solution.py:12
  372.8 2.9 collective-permute-start.9
  375.8 28.1 %collective-permute-start.10 = (f32[12,12,16,128]{3,2,0,1:T(8,128)S(1)}, f32[12,12,16,128]{3,2,0,1:T(8,128)}, u32[]{:S(2)}, u32[]{:S(2)}) collective-permute-start(f32[12,12,16,128]{3,2,0,1:T(8,128)S(1)} %collective-permute-done.9), channel_id=1, source_target_pairs={{0,8},{8,0},{16,24},{24,16},{1,9},{9,1},{17,25},{25,17},{2,10},{10... | collective-permute-start | bytes 3538952 | tf_op jit(solution)/shard_map/ppermute | solution.py:12
  404.0 28.6 %collective-permute-start.11 = (f32[12,12,16,128]{3,2,0,1:T(8,128)S(1)}, f32[12,12,16,128]{3,2,0,1:T(8,128)}, u32[]{:S(2)}, u32[]{:S(2)}) collective-permute-start(f32[12,12,16,128]{3,2,0,1:T(8,128)S(1)} %broadcast_select_fusion.2), channel_id=1, source_target_pairs={{0,64},{32,96},{64,0},{96,32},{1,65},{33,97},{65,1},{97,33},{2,66}... | collective-permute-start | bytes 3538952 | tf_op jit(solution)/shard_map/ppermute | solution.py:12
  432.6 29.3 %collective-permute-start.12 = (f32[12,12,16,128]{3,2,0,1:T(8,128)}, f32[12,12,16,128]{3,2,0,1:T(8,128)S(1)}, u32[]{:S(2)}, u32[]{:S(2)}) collective-permute-start(f32[12,12,16,128]{3,2,0,1:T(8,128)} %collective-permute-done.11), channel_id=1, source_target_pairs={{0,16},{8,24},{16,0},{24,8},{1,17},{9,25},{17,1},{25,9},{2,18},{10... | collective-permute-start | bytes 3538952 | tf_op jit(solution)/shard_map/ppermute | solution.py:12
Sparse Core Ops, SparseCore 0:
  11.9 94.3 all-gather.1

commit v4 on v3

--- a/solution.py
+++ b/solution.py
@@ -22,11 +22,14 @@
     return parity % 2 == 0
 
 
-def gather_row(ints):
+def gather_row(ints, row_at):
     zpart = shifted(ints, "row", lambda r: r ^ 2)
-    pair = jnp.stack([ints, zpart])
-    other = shifted(pair, "row", lambda r: r ^ 1)
-    return jnp.stack([ints, other[0], zpart, other[1]])
+    blocks = [ints, shifted(ints, "row", lambda r: r ^ 1), zpart, shifted(zpart, "row", lambda r: r ^ 1)]
+    k_rows = ints.shape[0]
+    whole = jnp.zeros((len(blocks) * k_rows,) + ints.shape[1:], ints.dtype)
+    for u, blk in enumerate(blocks):
+        whole = lax.dynamic_update_slice_in_dim(whole, blk, (row_at ^ u) * k_rows, axis=0)
+    return whole
 
 
 def ring_reduce_y(part, slab_at):
@@ -65,9 +68,7 @@
     ints = jnp.where(mask[None, :, None, :], integrals, jnp.zeros_like(integrals))
 
     amp_all = lax.all_gather(amp, "col", axis=1, tiled=True)
-    int_x = gather_row(ints)
-    order = jnp.arange(int_x.shape[0], dtype=jnp.int32) ^ row_at
-    int_abs = jnp.take(int_x, order, axis=0).reshape(amp_all.shape[1], c_cols, -1, win_cols)
+    int_abs = gather_row(ints, row_at)
     part = jnp.einsum("ikca,kcjb->ijab", amp_all, int_abs, preferred_element_type=jnp.float32)
 
     reduced_y = ring_reduce_y(part, slab_at)
@@ -77,8 +78,15 @@
     theirs = lax.dynamic_slice_in_dim(reduced_y, (1 - zh) * width, width, axis=2)
     shares = mine + shifted(theirs, "slab", lambda s: s ^ 1)
 
-    spread = lax.all_to_all(shares, "slab", 3, 2, tiled=True)
-    mirrored = jnp.transpose(spread, (1, 0, 3, 2))
+    i_n, j_n, a_n, b_n = shares.shape
+    mirrored = jnp.zeros((j_n, i_n, a_n, b_n), shares.dtype)
+    for d in range(n_slab):
+        tile = lax.dynamic_slice_in_dim(shares, (slab_at ^ d) * a_n, a_n, axis=3)
+        tile = jnp.transpose(tile, (1, 0, 3, 2))
+        if d:
+            flat = shifted(tile.reshape(j_n * i_n, a_n * a_n), "slab", lambda t, d=d: t ^ d)
+            tile = flat.reshape(j_n, i_n, a_n, a_n)
+        mirrored = lax.dynamic_update_slice_in_dim(mirrored, tile, (slab_at ^ d) * a_n, axis=3)
     for bit_no in range(lax.axis_size("row").bit_length() - 1):
         across = shifted(shifted(mirrored, "row", lambda r: r ^ 2**bit_no), "col", lambda c: c ^ 2**bit_no)
         differ = row_at // 2**bit_no % 2 != col_at // 2**bit_no % 2

time: 477 us -> 600 us (1.26)
  local copies, waits for them, and re-layouts: 114 us -> 261 us
  blocking collectives: 19.4 us -> 0 us
  starting transfers between devices: 23.6 us -> 35.8 us
  waiting for transfers between devices: 237 us -> 228 us
    dynamic_update_slice x0 -> x11, local copies, waits for them, and re-layouts: none -> 187 us  [the longest x8 175 us: body(): lax.dynamic_update_slice_in_dim(mirrored, tile, (slab_at ^ d) * a_n, axis=3)]
    reshape x0 -> x21, local copies, waits for them, and re-layouts: none -> 32.3 us  [the longest x7 16.5 us: body(): tile.reshape(j_n * i_n, a_n * a_n)]
    gather x12 -> x0, local copies, waits for them, and re-layouts: 29.1 us -> none
    transpose x0 -> x8, local copies, waits for them, and re-layouts: none -> 22.8 us  [body(): tile = jnp.transpose(tile, (1, 0, 3, 2))]
    unnamed x16 -> x19, local copies, waits for them, and re-layouts: 25.4 us -> 3.17 us
    all_to_all x3 -> x0, local copies, waits for them, and re-layouts: 20.7 us -> none  [body(): spread = lax.all_to_all(shares, 'slab', 3, 2, tiled=True)]
    all_to_all x1 -> x0, blocking collectives: 19.4 us -> none  [body(): spread = lax.all_to_all(shares, 'slab', 3, 2, tiled=True)]
    ppermute x13 -> x21, waiting for transfers between devices: 237 us -> 224 us  [shifted(): lax.ppermute(value, axis, [(src, fn(src) % size) for src in range(size)])]
  transfers between devices with their start and end apart: 14 -> 22, of which waited for: 12 -> 12; matrix products, arithmetic and copies ran while one was open for 17% -> 16% of each run, Pallas kernels for 0% -> 0%
where the time goes in v4:
time: 600 us; the launch traced here: 595 us
  local copies, waits for them, and re-layouts  261 us (44%)
  waiting for transfers between devices  228 us (38%)
  starting transfers between devices  35.8 us (6%)
  other arithmetic  33.7 us (6%)
  matrix products  19.7 us (3%)
  between operations  15.7 us (3%)
    ppermute x21, waiting for transfers between devices, shifted(): lax.ppermute(value, axis, [(src, fn(src) % size) for src in range(size)])  224 us
    dynamic_update_slice x8, local copies, waits for them, and re-layouts, body(): lax.dynamic_update_slice_in_dim(mirrored, tile, (slab_at ^ d) * a_n, axis=3)  175 us
    ppermute x21, starting transfers between devices, shifted(): lax.ppermute(value, axis, [(src, fn(src) % size) for src in range(size)])  35.8 us
    transpose x8, local copies, waits for them, and re-layouts, body(): tile = jnp.transpose(tile, (1, 0, 3, 2))  22.8 us
    dot_general x1, matrix products, body(): jnp.einsum('ikca,kcjb->ijab', amp_all, int_abs, preferred_element_type=jn...  19.7 us
    reshape x7, local copies, waits for them, and re-layouts, body(): tile.reshape(j_n * i_n, a_n * a_n)  16.5 us
    reshape x14, local copies, waits for them, and re-layouts, body(): tile = flat.reshape(j_n, i_n, a_n, a_n)  15.8 us
  transfers between devices with their start and end apart: 22, of which 12 were waited for; matrix products, arithmetic and copies ran while one was open for 16% of the time, Pallas kernels for 0%

profile of v4, /device:TPU:0, one launch (start us, length us, event | category | flops | bytes accessed | tf_op | source)
XLA Modules:
  0.0 594.6 jit_solution(181697261461673300)
XLA Ops:
  8.5 3.2 broadcast_select_fusion
  15.7 11.9 %and_select_fusion.1 = s32[128]{0:T(128)S(1)} fusion(s32[]{:T(128)} %bitcast.26, s32[]{:T(128)} %bitcast.27, s32[]{:T(128)} %bitcast.28, s32[]{:T(128)} %bitcast.29, s32[]{:T(128)} %bitcast.30, s32[]{:T(128)} %bitcast.32, s32[]{:T(128)} %bitcast.31, s32[]{:T(128)} %bitcast.3, s32[]{:T(128)} %bitcast.5, s32[]{:T(128)} %bitcast.7, s32[]{:T(128)} %bitcast.9, ...), kind=kLoop, calls=%fused_computation.67 | loop fusion | flops 8192 | bytes 588 | tf_op jit(solution)/shard_map/jit(_take)/select_n | solution.py:19
  31.4 51.5 %collective-permute-done.1 = bf16[12,60,12,128]{3,1,2,0:T(8,128)(2,1)} collective-permute-done((bf16[12,60,12,128]{3,1,2,0:T(8,128)(2,1)}, bf16[12,60,12,128]{3,1,2,0:T(8,128)(2,1)}, u32[]{:S(2)}, u32[]{:S(2)}) %collective-permute-start.1) | collective-permute-done | bytes 2211872 | tf_op jit(solution)/shard_map/ppermute | solution.py:12
  82.9 6.0 %broadcast_in_dim.35 = bf16[48,60,12,128]{3,1,0,2:T(8,128)(2,1)} broadcast(bf16[]{:T(256)} %constant.189.clone.1), dimensions={} | broadcast | bytes 8847362 | tf_op jit(solution)/shard_map/broadcast_in_dim | solution.py:29
  91.1 3.9 copy_dynamic-update-slice_fusion.2
  95.0 3.7 copy_dynamic-update-slice_fusion.1
  98.8 3.8 copy_dynamic-update-slice_fusion
  102.5 3.7 all-gather.2.cloned.1.call-done
  106.3 19.7 %fusion.3 = f32[12,12,128,128]{3,2,0,1:T(8,128)S(1)} fusion(bf16[12,48,60,128]{3,2,1,0:T(8,128)(2,1)} %all-gather.2.cloned.1.call-done, bf16[48,60,12,128]{3,1,0,2:T(8,128)(2,1)} %copy_dynamic-update-slice_fusion), kind=kOutput, calls=%fused_computation.4 | convolution fusion | flops 13589544960 | bytes 27131904 | tf_op jit(solution)/shard_map/ikca,kcjb->ijab/dot_general | solution.py:72
  126.0 3.2 fusion.16
  136.0 23.5 %collective-permute-done.6 = f32[6,12,32,128]{3,2,0,1:T(8,128)S(1)} collective-permute-done((f32[6,12,32,128]{3,2,0,1:T(8,128)S(1)}, f32[6,12,32,128]{3,2,0,1:T(8,128)S(1)}, u32[]{:S(2)}, u32[]{:S(2)}) %collective-permute-start.6) | collective-permute-done | bytes 1179680 | tf_op jit(solution)/shard_map/ppermute | solution.py:12
  161.0 3.8 collective-permute-start.7
  166.9 22.1 %collective-permute-done.7 = f32[6,12,32,128]{3,2,0,1:T(8,128)S(1)} collective-permute-done((f32[6,12,32,128]{3,2,0,1:T(8,128)S(1)}, f32[6,12,32,128]{3,2,0,1:T(8,128)S(1)}, u32[]{:S(2)}, u32[]{:S(2)}) %collective-permute-start.7) | collective-permute-done | bytes 1179680 | tf_op jit(solution)/shard_map/ppermute | solution.py:12
  190.5 3.8 collective-permute-start.8
  197.4 20.2 %collective-permute-done.8 = f32[6,12,32,128]{3,2,0,1:T(8,128)S(1)} collective-permute-done((f32[6,12,32,128]{3,2,0,1:T(8,128)S(1)}, f32[6,12,32,128]{3,2,0,1:T(8,128)S(1)}, u32[]{:S(2)}, u32[]{:S(2)}) %collective-permute-start.8) | collective-permute-done | bytes 1179680 | tf_op jit(solution)/shard_map/ppermute | solution.py:12
  219.2 5.4 collective-permute-done.5
  226.6 3.2 collective-permute-start.9
  229.8 23.2 %collective-permute-done.9 = f32[12,12,16,128]{3,2,0,1:T(8,128)} collective-permute-done((f32[12,12,16,128]{3,2,0,1:T(8,128)S(1)}, f32[12,12,16,128]{3,2,0,1:T(8,128)}, u32[]{:S(2)}, u32[]{:S(2)}) %collective-permute-start.9) | collective-permute-done | bytes 1179680 | tf_op jit(solution)/shard_map/ppermute | solution.py:12
  254.5 5.3 dynamic-slice_bitcast_fusion
  265.0 3.1 collective-permute-start.10
  290.0 6.1 %collective-permute-start.14 = (f32[144,256]{1,0:T(8,128)}, f32[144,256]{1,0:T(8,128)}, u32[]{:S(2)}, u32[]{:S(2)}) collective-permute-start(f32[144,256]{1,0:T(8,128)} %reshape.244), channel_id=1, source_target_pairs={{0,5},{1,4},{2,7},{3,6},{4,1},{5,0},{6,3},{7,2},{8,13},{9,12},{10,... | collective-permute-start | bytes 442376 | tf_op jit(solution)/shard_map/ppermute | solution.py:12
  309.6 6.1 %dynamic_update_slice.40 = f32[12,12,16,128]{3,2,0,1:T(8,128)} dynamic-update-slice(f32[12,12,16,128]{3,2,0,1:T(8,128)} %broadcast_in_dim.41, f32[12,12,16,16]{3,2,0,1:T(8,128)S(1)} %bitcast.145, s32[]{:T(128)} %constant.192.clone.1, s32[]{:T(128)} %constant.192.clone.1, s32[]{:T(128)} %constant.192.clone.1, s32[]{:T(128)S(6)} %select_n.318) | dynamic-update-slice | bytes 294916 | tf_op jit(solution)/shard_map/dynamic_update_slice | solution.py:89
  331.6 24.2 %dynamic_update_slice.41 = f32[12,12,16,128]{3,2,0,1:T(8,128)} dynamic-update-slice(f32[12,12,16,128]{3,2,0,1:T(8,128)} %dynamic_update_slice.40, f32[12,12,16,16]{3,2,0,1:T(8,128)S(1)} %copy.17, s32[]{:T(128)} %constant.192.clone.1, s32[]{:T(128)} %constant.192.clone.1, s32[]{:T(128)} %constant.192.clone.1, s32[]{:T(128)S(6)} %select_n.319) | dynamic-update-slice | bytes 294916 | tf_op jit(solution)/shard_map/dynamic_update_slice | solution.py:89
  355.8 24.2 %dynamic_update_slice.42 = f32[12,12,16,128]{3,2,0,1:T(8,128)} dynamic-update-slice(f32[12,12,16,128]{3,2,0,1:T(8,128)} %dynamic_update_slice.41, f32[12,12,16,16]{3,2,0,1:T(8,128)S(1)} %copy-done.3, s32[]{:T(128)} %constant.192.clone.1, s32[]{:T(128)} %constant.192.clone.1, s32[]{:T(128)} %constant.192.clone.1, s32[]{:T(128)S(6)} %select_n.320) | dynamic-update-slice | bytes 294916 | tf_op jit(solution)/shard_map/dynamic_update_slice | solution.py:89
  380.1 24.2 %dynamic_update_slice.43 = f32[12,12,16,128]{3,2,0,1:T(8,128)} dynamic-update-slice(f32[12,12,16,128]{3,2,0,1:T(8,128)} %dynamic_update_slice.42, f32[12,12,16,16]{3,2,0,1:T(8,128)S(1)} %copy-done.4, s32[]{:T(128)} %constant.192.clone.1, s32[]{:T(128)} %constant.192.clone.1, s32[]{:T(128)} %constant.192.clone.1, s32[]{:T(128)S(6)} %select_n.321) | dynamic-update-slice | bytes 294916 | tf_op jit(solution)/shard_map/dynamic_update_slice | solution.py:89
  404.3 24.2 %dynamic_update_slice.44 = f32[12,12,16,128]{3,2,0,1:T(8,128)} dynamic-update-slice(f32[12,12,16,128]{3,2,0,1:T(8,128)} %dynamic_update_slice.43, f32[12,12,16,16]{3,2,0,1:T(8,128)S(1)} %copy-done.5, s32[]{:T(128)} %constant.192.clone.1, s32[]{:T(128)} %constant.192.clone.1, s32[]{:T(128)} %constant.192.clone.1, s32[]{:T(128)S(6)} %select_n.322) | dynamic-update-slice | bytes 294916 | tf_op jit(solution)/shard_map/dynamic_update_slice | solution.py:89
  428.5 24.2 %dynamic_update_slice.45 = f32[12,12,16,128]{3,2,0,1:T(8,128)} dynamic-update-slice(f32[12,12,16,128]{3,2,0,1:T(8,128)} %dynamic_update_slice.44, f32[12,12,16,16]{3,2,0,1:T(8,128)S(1)} %copy-done.6, s32[]{:T(128)} %constant.192.clone.1, s32[]{:T(128)} %constant.192.clone.1, s32[]{:T(128)} %constant.192.clone.1, s32[]{:T(128)S(6)} %select_n.323) | dynamic-update-slice | bytes 294916 | tf_op jit(solution)/shard_map/dynamic_update_slice | solution.py:89
  452.8 24.2 %dynamic_update_slice.46 = f32[12,12,16,128]{3,2,0,1:T(8,128)} dynamic-update-slice(f32[12,12,16,128]{3,2,0,1:T(8,128)} %dynamic_update_slice.45, f32[12,12,16,16]{3,2,0,1:T(8,128)S(1)} %copy-done.7, s32[]{:T(128)} %constant.192.clone.1, s32[]{:T(128)} %constant.192.clone.1, s32[]{:T(128)} %constant.192.clone.1, s32[]{:T(128)S(6)} %select_n.324) | dynamic-update-slice | bytes 294916 | tf_op jit(solution)/shard_map/dynamic_update_slice | solution.py:89
  477.0 24.1 %dynamic_update_slice.47 = f32[12,12,16,128]{3,2,0,1:T(8,128)} dynamic-update-slice(f32[12,12,16,128]{3,2,0,1:T(8,128)} %dynamic_update_slice.46, f32[12,12,16,16]{3,2,0,1:T(8,128)S(1)} %copy-done.8, s32[]{:T(128)} %constant.192.clone.1, s32[]{:T(128)} %constant.192.clone.1, s32[]{:T(128)} %constant.192.clone.1, s32[]{:T(128)S(6)} %select_n.325) | dynamic-update-slice | bytes 294916 | tf_op jit(solution)/shard_map/dynamic_update_slice | solution.py:89
  505.6 26.6 %collective-permute-done.18 = f32[12,12,16,128]{3,2,0,1:T(8,128)S(1)} collective-permute-done((f32[12,12,16,128]{3,2,0,1:T(8,128)S(1)}, f32[12,12,16,128]{3,2,0,1:T(8,128)S(1)}, u32[]{:S(2)}, u32[]{:S(2)}) %collective-permute-start.18) | collective-permute-done | bytes 1179680 | tf_op jit(solution)/shard_map/ppermute | solution.py:12
  535.3 24.5 %collective-permute-done.19 = f32[12,12,16,128]{3,2,0,1:T(8,128)} collective-permute-done((f32[12,12,16,128]{3,2,0,1:T(8,128)S(1)}, f32[12,12,16,128]{3,2,0,1:T(8,128)}, u32[]{:S(2)}, u32[]{:S(2)}) %collective-permute-start.19) | collective-permute-done | bytes 1179680 | tf_op jit(solution)/shard_map/ppermute | solution.py:12
  562.4 24.1 %collective-permute-done.20 = f32[12,12,16,128]{3,2,0,1:T(8,128)S(1)} collective-permute-done((f32[12,12,16,128]{3,2,0,1:T(8,128)}, f32[12,12,16,128]{3,2,0,1:T(8,128)S(1)}, u32[]{:S(2)}, u32[]{:S(2)}) %collective-permute-start.20) | collective-permute-done | bytes 1179680 | tf_op jit(solution)/shard_map/ppermute | solution.py:12
  (101 shorter events, 97.8 us)
Async XLA Ops:
  6.5 99.7 %all-gather.2.cloned.1.call-start = ((), (), s32[]{:S(2)}) async-start(), calls=%async_computation | async-start | bytes 11796480 | tf_op jit(solution)/shard_map/all_gather | solution.py:70
  11.7 0.7 copy-start
  11.7 16.1 %copy-start.2 = (bf16[12,60,12,128]{3,1,2,0:T(8,128)(2,1)S(1)}, bf16[12,60,12,128]{3,1,2,0:T(8,128)(2,1)}, u32[]{:S(2)}) copy-start(bf16[12,60,12,128]{3,1,2,0:T(8,128)(2,1)} %param.5) | copy-start | bytes 6635524
  29.3 53.6 %collective-permute-start.1 = (bf16[12,60,12,128]{3,1,2,0:T(8,128)(2,1)}, bf16[12,60,12,128]{3,1,2,0:T(8,128)(2,1)}, u32[]{:S(2)}, u32[]{:S(2)}) collective-permute-start(bf16[12,60,12,128]{3,1,2,0:T(8,128)(2,1)} %broadcast_select_fusion.1), channel_id=1, source_target_pairs={{0,64},{32,96},{64,0},{96,32},{1,65},{33,97},{65,1},{97,33},{2,66}... | collective-permute-start | bytes 6635528 | tf_op jit(solution)/shard_map/ppermute | solution.py:12
  31.4 59.8 %collective-permute-start = (bf16[12,60,12,128]{3,1,2,0:T(8,128)(2,1)}, bf16[12,60,12,128]{3,1,2,0:T(8,128)(2,1)}, u32[]{:S(2)}, u32[]{:S(2)}) collective-permute-start(bf16[12,60,12,128]{3,1,2,0:T(8,128)(2,1)} %broadcast_select_fusion.1), channel_id=1, source_target_pairs={{0,32},{32,0},{64,96},{96,64},{1,33},{33,1},{65,97},{97,65},{2,34}... | collective-permute-start | bytes 6635528 | tf_op jit(solution)/shard_map/ppermute | solution.py:12
  82.9 15.9 %collective-permute-start.2 = (bf16[12,60,12,128]{3,1,2,0:T(8,128)(2,1)}, bf16[12,60,12,128]{3,1,2,0:T(8,128)(2,1)}, u32[]{:S(2)}, u32[]{:S(2)}) collective-permute-start(bf16[12,60,12,128]{3,1,2,0:T(8,128)(2,1)} %collective-permute-done.1), channel_id=1, source_target_pairs={{0,32},{32,0},{64,96},{96,64},{1,33},{33,1},{65,97},{97,65},{2,34}... | collective-permute-start | bytes 6635528 | tf_op jit(solution)/shard_map/ppermute | solution.py:12
  129.2 2.2 copy-start.1
  131.4 28.1 %collective-permute-start.6 = (f32[6,12,32,128]{3,2,0,1:T(8,128)S(1)}, f32[6,12,32,128]{3,2,0,1:T(8,128)S(1)}, u32[]{:S(2)}, u32[]{:S(2)}) collective-permute-start(f32[6,12,32,128]{3,2,0,1:T(8,128)S(1)} %constant_dynamic-slice_fusion.1), channel_id=1, source_target_pairs={{0,6},{1,7},{2,0},{3,1},{4,2},{5,3},{6,4},{7,5},{8,14},{9,15},{10,... | collective-permute-start | bytes 3538952 | tf_op jit(solution)/shard_map/ppermute | solution.py:12
  135.8 28.9 %collective-permute-start.3 = (f32[6,12,32,128]{3,2,0,1:T(8,128)S(1)}, f32[6,12,32,128]{3,2,0,1:T(8,128)}, u32[]{:S(2)}, u32[]{:S(2)}) collective-permute-start(f32[6,12,32,128]{3,2,0,1:T(8,128)S(1)} %constant_dynamic-slice_fusion.2), channel_id=1, source_target_pairs={{0,2},{1,3},{2,4},{3,5},{4,6},{5,7},{6,0},{7,1},{8,10},{9,11},{10,... | collective-permute-start | bytes 3538952 | tf_op jit(solution)/shard_map/ppermute | solution.py:12
  161.0 28.0 %collective-permute-start.7 = (f32[6,12,32,128]{3,2,0,1:T(8,128)S(1)}, f32[6,12,32,128]{3,2,0,1:T(8,128)S(1)}, u32[]{:S(2)}, u32[]{:S(2)}) collective-permute-start(f32[6,12,32,128]{3,2,0,1:T(8,128)S(1)} %dynamic-slice_add_fusion.2), channel_id=1, source_target_pairs={{0,6},{1,7},{2,0},{3,1},{4,2},{5,3},{6,4},{7,5},{8,14},{9,15},{10,... | collective-permute-start | bytes 3538952 | tf_op jit(solution)/shard_map/ppermute | solution.py:12
  166.7 27.8 %collective-permute-start.4 = (f32[6,12,32,128]{3,2,0,1:T(8,128)S(1)}, f32[6,12,32,128]{3,2,0,1:T(8,128)}, u32[]{:S(2)}, u32[]{:S(2)}) collective-permute-start(f32[6,12,32,128]{3,2,0,1:T(8,128)S(1)} %dynamic-slice_add_fusion.5), channel_id=1, source_target_pairs={{0,2},{1,3},{2,4},{3,5},{4,6},{5,7},{6,0},{7,1},{8,10},{9,11},{10,... | collective-permute-start | bytes 3538952 | tf_op jit(solution)/shard_map/ppermute | solution.py:12
  190.5 27.1 %collective-permute-start.8 = (f32[6,12,32,128]{3,2,0,1:T(8,128)S(1)}, f32[6,12,32,128]{3,2,0,1:T(8,128)S(1)}, u32[]{:S(2)}, u32[]{:S(2)}) collective-permute-start(f32[6,12,32,128]{3,2,0,1:T(8,128)S(1)} %dynamic-slice_add_fusion.1), channel_id=1, source_target_pairs={{0,6},{1,7},{2,0},{3,1},{4,2},{5,3},{6,4},{7,5},{8,14},{9,15},{10,... | collective-permute-start | bytes 3538952 | tf_op jit(solution)/shard_map/ppermute | solution.py:12
  197.4 27.1 %collective-permute-start.5 = (f32[6,12,32,128]{3,2,0,1:T(8,128)}, f32[6,12,32,128]{3,2,0,1:T(8,128)}, u32[]{:S(2)}, u32[]{:S(2)}) collective-permute-start(f32[6,12,32,128]{3,2,0,1:T(8,128)} %dynamic-slice_add_fusion.4), channel_id=1, source_target_pairs={{0,2},{1,3},{2,4},{3,5},{4,6},{5,7},{6,0},{7,1},{8,10},{9,11},{10,... | collective-permute-start | bytes 3538952 | tf_op jit(solution)/shard_map/ppermute | solution.py:12
  226.6 26.4 %collective-permute-start.9 = (f32[12,12,16,128]{3,2,0,1:T(8,128)S(1)}, f32[12,12,16,128]{3,2,0,1:T(8,128)}, u32[]{:S(2)}, u32[]{:S(2)}) collective-permute-start(f32[12,12,16,128]{3,2,0,1:T(8,128)S(1)} %fusion.8), channel_id=1, source_target_pairs={{0,1},{1,0},{2,3},{3,2},{4,5},{5,4},{6,7},{7,6},{8,9},{9,8},{10,11... | collective-permute-start | bytes 3538952 | tf_op jit(solution)/shard_map/ppermute | solution.py:12
  265.0 37.6 %collective-permute-start.10 = (f32[144,256]{1,0:T(8,128)}, f32[144,256]{1,0:T(8,128)}, u32[]{:S(2)}, u32[]{:S(2)}) collective-permute-start(f32[144,256]{1,0:T(8,128)} %reshape.236), channel_id=1, source_target_pairs={{0,1},{1,0},{2,3},{3,2},{4,5},{5,4},{6,7},{7,6},{8,9},{9,8},{10,11... | collective-permute-start | bytes 442376 | tf_op jit(solution)/shard_map/ppermute | solution.py:12
  273.1 31.8 %collective-permute-start.11 = (f32[144,256]{1,0:T(8,128)}, f32[144,256]{1,0:T(8,128)}, u32[]{:S(2)}, u32[]{:S(2)}) collective-permute-start(f32[144,256]{1,0:T(8,128)} %reshape.238), channel_id=1, source_target_pairs={{0,2},{1,3},{2,0},{3,1},{4,6},{5,7},{6,4},{7,5},{8,10},{9,11},{10,... | collective-permute-start | bytes 442376 | tf_op jit(solution)/shard_map/ppermute | solution.py:12
  278.1 41.4 %collective-permute-start.12 = (f32[144,256]{1,0:T(8,128)}, f32[144,256]{1,0:T(8,128)}, u32[]{:S(2)}, u32[]{:S(2)}) collective-permute-start(f32[144,256]{1,0:T(8,128)} %reshape.240), channel_id=1, source_target_pairs={{0,3},{1,2},{2,1},{3,0},{4,7},{5,6},{6,5},{7,4},{8,11},{9,10},{10,... | collective-permute-start | bytes 442376 | tf_op jit(solution)/shard_map/ppermute | solution.py:12
  285.0 36.9 %collective-permute-start.13 = (f32[144,256]{1,0:T(8,128)}, f32[144,256]{1,0:T(8,128)}, u32[]{:S(2)}, u32[]{:S(2)}) collective-permute-start(f32[144,256]{1,0:T(8,128)} %reshape.242), channel_id=1, source_target_pairs={{0,4},{1,5},{2,6},{3,7},{4,0},{5,1},{6,2},{7,3},{8,12},{9,13},{10,... | collective-permute-start | bytes 442376 | tf_op jit(solution)/shard_map/ppermute | solution.py:12
  290.0 34.3 %collective-permute-start.14 = (f32[144,256]{1,0:T(8,128)}, f32[144,256]{1,0:T(8,128)}, u32[]{:S(2)}, u32[]{:S(2)}) collective-permute-start(f32[144,256]{1,0:T(8,128)} %reshape.244), channel_id=1, source_target_pairs={{0,5},{1,4},{2,7},{3,6},{4,1},{5,0},{6,3},{7,2},{8,13},{9,12},{10,... | collective-permute-start | bytes 442376 | tf_op jit(solution)/shard_map/ppermute | solution.py:12
  302.5 24.2 %collective-permute-start.15 = (f32[144,256]{1,0:T(8,128)}, f32[144,256]{1,0:T(8,128)}, u32[]{:S(2)}, u32[]{:S(2)}) collective-permute-start(f32[144,256]{1,0:T(8,128)} %reshape.246), channel_id=1, source_target_pairs={{0,6},{1,7},{2,4},{3,5},{4,2},{5,3},{6,0},{7,1},{8,14},{9,15},{10,... | collective-permute-start | bytes 442376 | tf_op jit(solution)/shard_map/ppermute | solution.py:12
  304.9 24.3 %collective-permute-start.16 = (f32[144,256]{1,0:T(8,128)}, f32[144,256]{1,0:T(8,128)}, u32[]{:S(2)}, u32[]{:S(2)}) collective-permute-start(f32[144,256]{1,0:T(8,128)} %reshape.248), channel_id=1, source_target_pairs={{0,7},{1,6},{2,5},{3,4},{4,3},{5,2},{6,1},{7,0},{8,15},{9,14},{10,... | collective-permute-start | bytes 442376 | tf_op jit(solution)/shard_map/ppermute | solution.py:12
  331.6 24.2 %copy-start.3 = (f32[12,12,16,16]{3,2,0,1:T(8,128)S(1)}, f32[12,12,16,16]{3,2,0,1:T(8,128)}, u32[]{:S(2)}) copy-start(f32[12,12,16,16]{3,2,0,1:T(8,128)} %copy.19) | copy-start | bytes 442372
  355.8 24.2 %copy-start.4 = (f32[12,12,16,16]{3,2,0,1:T(8,128)S(1)}, f32[12,12,16,16]{3,2,0,1:T(8,128)}, u32[]{:S(2)}) copy-start(f32[12,12,16,16]{3,2,0,1:T(8,128)} %copy.21) | copy-start | bytes 442372
  380.0 24.2 %copy-start.5 = (f32[12,12,16,16]{3,2,0,1:T(8,128)S(1)}, f32[12,12,16,16]{3,2,0,1:T(8,128)}, u32[]{:S(2)}) copy-start(f32[12,12,16,16]{3,2,0,1:T(8,128)} %copy.23) | copy-start | bytes 442372
  404.3 24.2 %copy-start.6 = (f32[12,12,16,16]{3,2,0,1:T(8,128)S(1)}, f32[12,12,16,16]{3,2,0,1:T(8,128)}, u32[]{:S(2)}) copy-start(f32[12,12,16,16]{3,2,0,1:T(8,128)} %copy.25) | copy-start | bytes 442372
  428.5 24.2 %copy-start.7 = (f32[12,12,16,16]{3,2,0,1:T(8,128)S(1)}, f32[12,12,16,16]{3,2,0,1:T(8,128)}, u32[]{:S(2)}) copy-start(f32[12,12,16,16]{3,2,0,1:T(8,128)} %copy.27) | copy-start | bytes 442372
  452.8 24.2 %copy-start.8 = (f32[12,12,16,16]{3,2,0,1:T(8,128)S(1)}, f32[12,12,16,16]{3,2,0,1:T(8,128)}, u32[]{:S(2)}) copy-start(f32[12,12,16,16]{3,2,0,1:T(8,128)} %copy.29) | copy-start | bytes 442372
  501.1 3.1 collective-permute-start.17
  504.3 28.0 %collective-permute-start.18 = (f32[12,12,16,128]{3,2,0,1:T(8,128)S(1)}, f32[12,12,16,128]{3,2,0,1:T(8,128)S(1)}, u32[]{:S(2)}, u32[]{:S(2)}) collective-permute-start(f32[12,12,16,128]{3,2,0,1:T(8,128)S(1)} %collective-permute-done.17), channel_id=1, source_target_pairs={{0,8},{8,0},{16,24},{24,16},{1,9},{9,1},{17,25},{25,17},{2,10},{10... | collective-permute-start | bytes 3538952 | tf_op jit(solution)/shard_map/ppermute | solution.py:12
  533.7 26.1 %collective-permute-start.19 = (f32[12,12,16,128]{3,2,0,1:T(8,128)S(1)}, f32[12,12,16,128]{3,2,0,1:T(8,128)}, u32[]{:S(2)}, u32[]{:S(2)}) collective-permute-start(f32[12,12,16,128]{3,2,0,1:T(8,128)S(1)} %broadcast_select_fusion.2), channel_id=1, source_target_pairs={{0,64},{32,96},{64,0},{96,32},{1,65},{33,97},{65,1},{97,33},{2,66}... | collective-permute-start | bytes 3538952 | tf_op jit(solution)/shard_map/ppermute | solution.py:12
  559.8 26.7 %collective-permute-start.20 = (f32[12,12,16,128]{3,2,0,1:T(8,128)}, f32[12,12,16,128]{3,2,0,1:T(8,128)S(1)}, u32[]{:S(2)}, u32[]{:S(2)}) collective-permute-start(f32[12,12,16,128]{3,2,0,1:T(8,128)} %collective-permute-done.19), channel_id=1, source_target_pairs={{0,16},{8,24},{16,0},{24,8},{1,17},{9,25},{17,1},{25,9},{2,18},{10... | collective-permute-start | bytes 3538952 | tf_op jit(solution)/shard_map/ppermute | solution.py:12
Sparse Core Ops, SparseCore 0:
  11.8 94.3 all-gather.1

commit v5 on v4

--- a/solution.py
+++ b/solution.py
@@ -79,14 +79,15 @@
     shares = mine + shifted(theirs, "slab", lambda s: s ^ 1)
 
     i_n, j_n, a_n, b_n = shares.shape
-    mirrored = jnp.zeros((j_n, i_n, a_n, b_n), shares.dtype)
+    gathered = jnp.zeros((n_slab, j_n * i_n, a_n * a_n), shares.dtype)
     for d in range(n_slab):
         tile = lax.dynamic_slice_in_dim(shares, (slab_at ^ d) * a_n, a_n, axis=3)
-        tile = jnp.transpose(tile, (1, 0, 3, 2))
+        flat = jnp.transpose(tile, (1, 0, 3, 2)).reshape(1, j_n * i_n, a_n * a_n)
         if d:
-            flat = shifted(tile.reshape(j_n * i_n, a_n * a_n), "slab", lambda t, d=d: t ^ d)
-            tile = flat.reshape(j_n, i_n, a_n, a_n)
-        mirrored = lax.dynamic_update_slice_in_dim(mirrored, tile, (slab_at ^ d) * a_n, axis=3)
+            flat = shifted(flat, "slab", lambda t, d=d: t ^ d)
+        gathered = lax.dynamic_update_slice_in_dim(gathered, flat, slab_at ^ d, axis=0)
+    gathered = gathered.reshape(n_slab, j_n, i_n, a_n, a_n)
+    mirrored = jnp.transpose(gathered, (1, 2, 3, 0, 4)).reshape(j_n, i_n, a_n, b_n)
     for bit_no in range(lax.axis_size("row").bit_length() - 1):
         across = shifted(shifted(mirrored, "row", lambda r: r ^ 2**bit_no), "col", lambda c: c ^ 2**bit_no)
         differ = row_at // 2**bit_no % 2 != col_at // 2**bit_no % 2

time: 600 us -> 444 us (0.74)
  local copies, waits for them, and re-layouts: 261 us -> 106 us
    dynamic_update_slice x8, local copies, waits for them, and re-layouts: 175 us -> 9.88 us  [body(): lax.dynamic_update_slice_in_dim(gathered, flat, slab_at ^ d, axis=0)]
    transpose x8 -> x10, local copies, waits for them, and re-layouts: 22.8 us -> 36 us  [the longest x9 23.2 us: body(): flat = jnp.transpose(tile, (1, 0, 3, 2)).reshape(1, j_n * i_n, a_n * a_n)]
    reshape x21 -> x10, local copies, waits for them, and re-layouts: 32.3 us -> 29.7 us  [the longest x8 16.9 us: body(): flat = jnp.transpose(tile, (1, 0, 3, 2)).reshape(1, j_n * i_n, a_n * a_n)]
  transfers between devices with their start and end apart: 22 -> 22, of which waited for: 12 -> 12; matrix products, arithmetic and copies ran while one was open for 16% -> 19% of each run, Pallas kernels for 0% -> 0%
where the time goes in v5:
time: 444 us; the launch traced here: 443 us
  waiting for transfers between devices  233 us (52%)
  local copies, waits for them, and re-layouts  106 us (24%)
  starting transfers between devices  37.6 us (8%)
  other arithmetic  30.6 us (7%)
  matrix products  19.7 us (4%)
  between operations  15.6 us (4%)
    ppermute x21, waiting for transfers between devices, shifted(): lax.ppermute(value, axis, [(src, fn(src) % size) for src in range(size)])  229 us
    ppermute x21, starting transfers between devices, shifted(): lax.ppermute(value, axis, [(src, fn(src) % size) for src in range(size)])  37.6 us
    transpose x9, local copies, waits for them, and re-layouts, body(): flat = jnp.transpose(tile, (1, 0, 3, 2)).reshape(1, j_n * i_n, a_n * a_n)  23.2 us
    dot_general x1, matrix products, body(): jnp.einsum('ikca,kcjb->ijab', amp_all, int_abs, preferred_element_type=jn...  19.7 us
    reshape x8, local copies, waits for them, and re-layouts, body(): flat = jnp.transpose(tile, (1, 0, 3, 2)).reshape(1, j_n * i_n, a_n * a_n)  16.9 us
    transpose x1, local copies, waits for them, and re-layouts, body(): jnp.transpose(gathered, (1, 2, 3, 0, 4)).reshape(j_n, i_n, a_n, b_n)  12.8 us
    select_n x1, other arithmetic, int_mask(): label_b = jnp.take(irreps, blocks + b_ids // VTILE)  11.9 us
    dynamic_update_slice x3, local copies, waits for them, and re-layouts, gather_row(): lax.dynamic_update_slice_in_dim(whole, blk, (row_at ^ u) * k_rows, axis=0)  11.4 us
  transfers between devices with their start and end apart: 22, of which 12 were waited for; matrix products, arithmetic and copies ran while one was open for 19% of the time, Pallas kernels for 0%

profile of v5, /device:TPU:0, one launch (start us, length us, event | category | flops | bytes accessed | tf_op | source)
XLA Modules:
  0.0 442.9 jit_solution(17522962651929483631)
XLA Ops:
  14.1 11.9 %and_select_fusion.1 = s32[128]{0:T(128)S(1)} fusion(s32[]{:T(128)} %bitcast.26, s32[]{:T(128)} %bitcast.27, s32[]{:T(128)} %bitcast.28, s32[]{:T(128)} %bitcast.29, s32[]{:T(128)} %bitcast.30, s32[]{:T(128)} %bitcast.32, s32[]{:T(128)} %bitcast.31, s32[]{:T(128)} %bitcast.3, s32[]{:T(128)} %bitcast.5, s32[]{:T(128)} %bitcast.7, s32[]{:T(128)} %bitcast.9, ...), kind=kLoop, calls=%fused_computation.75 | loop fusion | flops 8192 | bytes 588 | tf_op jit(solution)/shard_map/jit(_take)/select_n | solution.py:19
  27.7 3.7 collective-permute-start.1
  31.4 51.6 %collective-permute-done.1 = bf16[12,60,12,128]{3,1,2,0:T(8,128)(2,1)} collective-permute-done((bf16[12,60,12,128]{3,1,2,0:T(8,128)(2,1)}, bf16[12,60,12,128]{3,1,2,0:T(8,128)(2,1)}, u32[]{:S(2)}, u32[]{:S(2)}) %collective-permute-start.1) | collective-permute-done | bytes 2211872 | tf_op jit(solution)/shard_map/ppermute | solution.py:12
  82.9 6.0 %broadcast_in_dim.35 = bf16[48,60,12,128]{3,1,0,2:T(8,128)(2,1)} broadcast(bf16[]{:T(256)} %constant.190.clone.1), dimensions={} | broadcast | bytes 8847362 | tf_op jit(solution)/shard_map/broadcast_in_dim | solution.py:29
  91.1 3.8 copy_dynamic-update-slice_fusion.2
  94.9 3.8 copy_dynamic-update-slice_fusion.1
  98.7 3.8 copy_dynamic-update-slice_fusion
  102.5 3.8 all-gather.2.cloned.1.call-done
  106.3 19.7 %fusion.3 = f32[12,12,128,128]{3,2,0,1:T(8,128)S(1)} fusion(bf16[12,48,60,128]{3,2,1,0:T(8,128)(2,1)} %all-gather.2.cloned.1.call-done, bf16[48,60,12,128]{3,1,0,2:T(8,128)(2,1)} %copy_dynamic-update-slice_fusion), kind=kOutput, calls=%fused_computation.4 | convolution fusion | flops 13589544960 | bytes 27131904 | tf_op jit(solution)/shard_map/ikca,kcjb->ijab/dot_general | solution.py:72
  126.0 3.2 fusion.16
  131.4 3.0 collective-permute-start.6
  136.0 23.5 %collective-permute-done.6 = f32[6,12,32,128]{3,2,0,1:T(8,128)S(1)} collective-permute-done((f32[6,12,32,128]{3,2,0,1:T(8,128)S(1)}, f32[6,12,32,128]{3,2,0,1:T(8,128)S(1)}, u32[]{:S(2)}, u32[]{:S(2)}) %collective-permute-start.6) | collective-permute-done | bytes 1179680 | tf_op jit(solution)/shard_map/ppermute | solution.py:12
  161.0 3.8 collective-permute-start.7
  166.9 22.1 %collective-permute-done.7 = f32[6,12,32,128]{3,2,0,1:T(8,128)S(1)} collective-permute-done((f32[6,12,32,128]{3,2,0,1:T(8,128)S(1)}, f32[6,12,32,128]{3,2,0,1:T(8,128)S(1)}, u32[]{:S(2)}, u32[]{:S(2)}) %collective-permute-start.7) | collective-permute-done | bytes 1179680 | tf_op jit(solution)/shard_map/ppermute | solution.py:12
  190.5 3.8 collective-permute-start.8
  194.5 2.9 dynamic-slice_add_fusion.4
  197.4 20.2 %collective-permute-done.8 = f32[6,12,32,128]{3,2,0,1:T(8,128)S(1)} collective-permute-done((f32[6,12,32,128]{3,2,0,1:T(8,128)S(1)}, f32[6,12,32,128]{3,2,0,1:T(8,128)S(1)}, u32[]{:S(2)}, u32[]{:S(2)}) %collective-permute-start.8) | collective-permute-done | bytes 1179680 | tf_op jit(solution)/shard_map/ppermute | solution.py:12
  219.1 5.4 %collective-permute-done.5 = f32[6,12,32,128]{3,2,0,1:T(8,128)} collective-permute-done((f32[6,12,32,128]{3,2,0,1:T(8,128)}, f32[6,12,32,128]{3,2,0,1:T(8,128)}, u32[]{:S(2)}, u32[]{:S(2)}) %collective-permute-start.5) | collective-permute-done | bytes 1179680 | tf_op jit(solution)/shard_map/ppermute | solution.py:12
  226.6 3.2 collective-permute-start.9
  229.8 23.1 %collective-permute-done.9 = f32[12,12,16,128]{3,2,0,1:T(8,128)} collective-permute-done((f32[12,12,16,128]{3,2,0,1:T(8,128)S(1)}, f32[12,12,16,128]{3,2,0,1:T(8,128)}, u32[]{:S(2)}, u32[]{:S(2)}) %collective-permute-start.9) | collective-permute-done | bytes 1179680 | tf_op jit(solution)/shard_map/ppermute | solution.py:12
  254.5 5.3 %dynamic-slice_bitcast_fusion = (f32[12,12,16,16]{2,3,1,0:T(8,128)S(1)}, f32[12,12,16,16]{2,3,1,0:T(8,128)S(1)}, f32[12,12,16,16]{2,3,1,0:T(8,128)}, f32[12,12,1...) fusion(f32[12,12,16,128]{3,2,0,1:T(8,128)S(1)} %fusion.10, ...), kind=kLoop, calls=%fused_computation.19 | loop fusion | bytes 2359328 | tf_op jit(solution)/shard_map/transpose | solution.py:85
  259.8 2.7 copy.15
  264.9 3.2 collective-permute-start.10
  295.0 6.2 %collective-permute-start.14 = (f32[1,144,256]{2,1,0:T(8,128)}, f32[1,144,256]{2,1,0:T(8,128)}, u32[]{:S(2)}, u32[]{:S(2)}) collective-permute-start(f32[1,144,256]{2,1,0:T(8,128)} %reshape.229), channel_id=1, source_target_pairs={{0,5},{1,4},{2,7},{3,6},{4,1},{5,0},{6,3},{7,2},{8,13},{9,12},{10,... | collective-permute-start | bytes 442376 | tf_op jit(solution)/shard_map/ppermute | solution.py:12
  309.6 3.0 collective-permute-start.16
  320.3 6.5 %reshape.232 = f32[8,12,12,16,16]{4,3,2,1,0:T(8,128)} reshape(f32[8,144,256]{2,1,0:T(8,128)} %constant_dynamic-update-slice_fusion) | data formatting | bytes 2359296 | tf_op jit(solution)/shard_map/reshape | solution.py:89
  326.8 12.8 %copy.22 = f32[12,12,16,8,16]{4,3,2,0,1:T(8,128)} copy(f32[12,12,16,8,16]{4,2,1,0,3:T(8,128)} %bitcast.153) | data formatting | bytes 2359296 | tf_op jit(solution)/shard_map/transpose | solution.py:90
  339.6 6.2 %reshape.233 = f32[12,12,16,128]{3,2,0,1:T(8,128)S(1)} reshape(f32[12,12,16,8,16]{4,3,2,0,1:T(8,128)} %copy.22) | data formatting | bytes 2359296 | tf_op jit(solution)/shard_map/reshape | solution.py:90
  345.9 2.8 collective-permute-done.17
  350.2 26.7 %collective-permute-done.18 = f32[12,12,16,128]{3,2,0,1:T(8,128)} collective-permute-done((f32[12,12,16,128]{3,2,0,1:T(8,128)S(1)}, f32[12,12,16,128]{3,2,0,1:T(8,128)}, u32[]{:S(2)}, u32[]{:S(2)}) %collective-permute-start.18) | collective-permute-done | bytes 1179680 | tf_op jit(solution)/shard_map/ppermute | solution.py:12
  378.6 27.0 %collective-permute-done.19 = f32[12,12,16,128]{3,2,0,1:T(8,128)} collective-permute-done((f32[12,12,16,128]{3,2,0,1:T(8,128)S(1)}, f32[12,12,16,128]{3,2,0,1:T(8,128)}, u32[]{:S(2)}, u32[]{:S(2)}) %collective-permute-start.19) | collective-permute-done | bytes 1179680 | tf_op jit(solution)/shard_map/ppermute | solution.py:12
  408.3 26.6 %collective-permute-done.20 = f32[12,12,16,128]{3,2,0,1:T(8,128)S(1)} collective-permute-done((f32[12,12,16,128]{3,2,0,1:T(8,128)}, f32[12,12,16,128]{3,2,0,1:T(8,128)S(1)}, u32[]{:S(2)}, u32[]{:S(2)}) %collective-permute-start.20) | collective-permute-done | bytes 1179680 | tf_op jit(solution)/shard_map/ppermute | solution.py:12
  (83 shorter events, 76.1 us)
Async XLA Ops:
  6.5 99.7 %all-gather.2.cloned.1.call-start = ((), (), s32[]{:S(2)}) async-start(), calls=%async_computation | async-start | bytes 11796480 | tf_op jit(solution)/shard_map/all_gather | solution.py:70
  10.0 0.7 copy-start
  10.0 16.1 %copy-start.2 = (bf16[12,60,12,128]{3,1,2,0:T(8,128)(2,1)S(1)}, bf16[12,60,12,128]{3,1,2,0:T(8,128)(2,1)}, u32[]{:S(2)}) copy-start(bf16[12,60,12,128]{3,1,2,0:T(8,128)(2,1)} %param.5) | copy-start | bytes 6635524
  27.7 55.3 %collective-permute-start.1 = (bf16[12,60,12,128]{3,1,2,0:T(8,128)(2,1)}, bf16[12,60,12,128]{3,1,2,0:T(8,128)(2,1)}, u32[]{:S(2)}, u32[]{:S(2)}) collective-permute-start(bf16[12,60,12,128]{3,1,2,0:T(8,128)(2,1)} %broadcast_select_fusion.1), channel_id=1, source_target_pairs={{0,64},{32,96},{64,0},{96,32},{1,65},{33,97},{65,1},{97,33},{2,66}... | collective-permute-start | bytes 6635528 | tf_op jit(solution)/shard_map/ppermute | solution.py:12
  31.4 59.7 %collective-permute-start = (bf16[12,60,12,128]{3,1,2,0:T(8,128)(2,1)}, bf16[12,60,12,128]{3,1,2,0:T(8,128)(2,1)}, u32[]{:S(2)}, u32[]{:S(2)}) collective-permute-start(bf16[12,60,12,128]{3,1,2,0:T(8,128)(2,1)} %broadcast_select_fusion.1), channel_id=1, source_target_pairs={{0,32},{32,0},{64,96},{96,64},{1,33},{33,1},{65,97},{97,65},{2,34}... | collective-permute-start | bytes 6635528 | tf_op jit(solution)/shard_map/ppermute | solution.py:12
  82.9 15.8 %collective-permute-start.2 = (bf16[12,60,12,128]{3,1,2,0:T(8,128)(2,1)}, bf16[12,60,12,128]{3,1,2,0:T(8,128)(2,1)}, u32[]{:S(2)}, u32[]{:S(2)}) collective-permute-start(bf16[12,60,12,128]{3,1,2,0:T(8,128)(2,1)} %collective-permute-done.1), channel_id=1, source_target_pairs={{0,32},{32,0},{64,96},{96,64},{1,33},{33,1},{65,97},{97,65},{2,34}... | collective-permute-start | bytes 6635528 | tf_op jit(solution)/shard_map/ppermute | solution.py:12
  129.2 2.2 copy-start.1
  131.4 28.1 %collective-permute-start.6 = (f32[6,12,32,128]{3,2,0,1:T(8,128)S(1)}, f32[6,12,32,128]{3,2,0,1:T(8,128)S(1)}, u32[]{:S(2)}, u32[]{:S(2)}) collective-permute-start(f32[6,12,32,128]{3,2,0,1:T(8,128)S(1)} %constant_dynamic-slice_fusion), channel_id=1, source_target_pairs={{0,6},{1,7},{2,0},{3,1},{4,2},{5,3},{6,4},{7,5},{8,14},{9,15},{10,... | collective-permute-start | bytes 3538952 | tf_op jit(solution)/shard_map/ppermute | solution.py:12
  135.8 28.9 %collective-permute-start.3 = (f32[6,12,32,128]{3,2,0,1:T(8,128)S(1)}, f32[6,12,32,128]{3,2,0,1:T(8,128)}, u32[]{:S(2)}, u32[]{:S(2)}) collective-permute-start(f32[6,12,32,128]{3,2,0,1:T(8,128)S(1)} %constant_dynamic-slice_fusion.1), channel_id=1, source_target_pairs={{0,2},{1,3},{2,4},{3,5},{4,6},{5,7},{6,0},{7,1},{8,10},{9,11},{10,... | collective-permute-start | bytes 3538952 | tf_op jit(solution)/shard_map/ppermute | solution.py:12
  161.0 28.0 %collective-permute-start.7 = (f32[6,12,32,128]{3,2,0,1:T(8,128)S(1)}, f32[6,12,32,128]{3,2,0,1:T(8,128)S(1)}, u32[]{:S(2)}, u32[]{:S(2)}) collective-permute-start(f32[6,12,32,128]{3,2,0,1:T(8,128)S(1)} %dynamic-slice_add_fusion.2), channel_id=1, source_target_pairs={{0,6},{1,7},{2,0},{3,1},{4,2},{5,3},{6,4},{7,5},{8,14},{9,15},{10,... | collective-permute-start | bytes 3538952 | tf_op jit(solution)/shard_map/ppermute | solution.py:12
  166.7 27.8 %collective-permute-start.4 = (f32[6,12,32,128]{3,2,0,1:T(8,128)S(1)}, f32[6,12,32,128]{3,2,0,1:T(8,128)}, u32[]{:S(2)}, u32[]{:S(2)}) collective-permute-start(f32[6,12,32,128]{3,2,0,1:T(8,128)S(1)} %dynamic-slice_add_fusion.5), channel_id=1, source_target_pairs={{0,2},{1,3},{2,4},{3,5},{4,6},{5,7},{6,0},{7,1},{8,10},{9,11},{10,... | collective-permute-start | bytes 3538952 | tf_op jit(solution)/shard_map/ppermute | solution.py:12
  190.5 27.1 %collective-permute-start.8 = (f32[6,12,32,128]{3,2,0,1:T(8,128)S(1)}, f32[6,12,32,128]{3,2,0,1:T(8,128)S(1)}, u32[]{:S(2)}, u32[]{:S(2)}) collective-permute-start(f32[6,12,32,128]{3,2,0,1:T(8,128)S(1)} %dynamic-slice_add_fusion.1), channel_id=1, source_target_pairs={{0,6},{1,7},{2,0},{3,1},{4,2},{5,3},{6,4},{7,5},{8,14},{9,15},{10,... | collective-permute-start | bytes 3538952 | tf_op jit(solution)/shard_map/ppermute | solution.py:12
  197.4 27.1 %collective-permute-start.5 = (f32[6,12,32,128]{3,2,0,1:T(8,128)}, f32[6,12,32,128]{3,2,0,1:T(8,128)}, u32[]{:S(2)}, u32[]{:S(2)}) collective-permute-start(f32[6,12,32,128]{3,2,0,1:T(8,128)} %dynamic-slice_add_fusion.4), channel_id=1, source_target_pairs={{0,2},{1,3},{2,4},{3,5},{4,6},{5,7},{6,0},{7,1},{8,10},{9,11},{10,... | collective-permute-start | bytes 3538952 | tf_op jit(solution)/shard_map/ppermute | solution.py:12
  226.6 26.4 %collective-permute-start.9 = (f32[12,12,16,128]{3,2,0,1:T(8,128)S(1)}, f32[12,12,16,128]{3,2,0,1:T(8,128)}, u32[]{:S(2)}, u32[]{:S(2)}) collective-permute-start(f32[12,12,16,128]{3,2,0,1:T(8,128)S(1)} %fusion.8), channel_id=1, source_target_pairs={{0,1},{1,0},{2,3},{3,2},{4,5},{5,4},{6,7},{7,6},{8,9},{9,8},{10,11... | collective-permute-start | bytes 3538952 | tf_op jit(solution)/shard_map/ppermute | solution.py:12
  264.9 42.7 %collective-permute-start.10 = (f32[1,144,256]{2,1,0:T(8,128)}, f32[1,144,256]{2,1,0:T(8,128)}, u32[]{:S(2)}, u32[]{:S(2)}) collective-permute-start(f32[1,144,256]{2,1,0:T(8,128)} %reshape.225), channel_id=1, source_target_pairs={{0,1},{1,0},{2,3},{3,2},{4,5},{5,4},{6,7},{7,6},{8,9},{9,8},{10,11... | collective-permute-start | bytes 442376 | tf_op jit(solution)/shard_map/ppermute | solution.py:12
  278.2 31.4 %collective-permute-start.11 = (f32[1,144,256]{2,1,0:T(8,128)}, f32[1,144,256]{2,1,0:T(8,128)}, u32[]{:S(2)}, u32[]{:S(2)}) collective-permute-start(f32[1,144,256]{2,1,0:T(8,128)} %reshape.226), channel_id=1, source_target_pairs={{0,2},{1,3},{2,0},{3,1},{4,6},{5,7},{6,4},{7,5},{8,10},{9,11},{10,... | collective-permute-start | bytes 442376 | tf_op jit(solution)/shard_map/ppermute | solution.py:12
  283.2 31.0 %collective-permute-start.12 = (f32[1,144,256]{2,1,0:T(8,128)}, f32[1,144,256]{2,1,0:T(8,128)}, u32[]{:S(2)}, u32[]{:S(2)}) collective-permute-start(f32[1,144,256]{2,1,0:T(8,128)} %reshape.227), channel_id=1, source_target_pairs={{0,3},{1,2},{2,1},{3,0},{4,7},{5,6},{6,5},{7,4},{8,11},{9,10},{10,... | collective-permute-start | bytes 442376 | tf_op jit(solution)/shard_map/ppermute | solution.py:12
  290.0 25.8 %collective-permute-start.13 = (f32[1,144,256]{2,1,0:T(8,128)}, f32[1,144,256]{2,1,0:T(8,128)}, u32[]{:S(2)}, u32[]{:S(2)}) collective-permute-start(f32[1,144,256]{2,1,0:T(8,128)} %reshape.228), channel_id=1, source_target_pairs={{0,4},{1,5},{2,6},{3,7},{4,0},{5,1},{6,2},{7,3},{8,12},{9,13},{10,... | collective-permute-start | bytes 442376 | tf_op jit(solution)/shard_map/ppermute | solution.py:12
  295.0 7.3 %copy-start.3 = (f32[1,144,256]{2,1,0:T(8,128)S(1)}, f32[1,144,256]{2,1,0:T(8,128)}, u32[]{:S(2)}) copy-start(f32[1,144,256]{2,1,0:T(8,128)} %reshape.224) | copy-start | bytes 442372
  295.0 22.3 %collective-permute-start.14 = (f32[1,144,256]{2,1,0:T(8,128)}, f32[1,144,256]{2,1,0:T(8,128)}, u32[]{:S(2)}, u32[]{:S(2)}) collective-permute-start(f32[1,144,256]{2,1,0:T(8,128)} %reshape.229), channel_id=1, source_target_pairs={{0,5},{1,4},{2,7},{3,6},{4,1},{5,0},{6,3},{7,2},{8,13},{9,12},{10,... | collective-permute-start | bytes 442376 | tf_op jit(solution)/shard_map/ppermute | solution.py:12
  307.1 0.9 copy-start.4
  308.0 10.9 %collective-permute-start.15 = (f32[1,144,256]{2,1,0:T(8,128)S(1)}, f32[1,144,256]{2,1,0:T(8,128)S(1)}, u32[]{:S(2)}, u32[]{:S(2)}) collective-permute-start(f32[1,144,256]{2,1,0:T(8,128)S(1)} %copy-done.4), channel_id=1, source_target_pairs={{0,6},{1,7},{2,4},{3,5},{4,2},{5,3},{6,0},{7,1},{8,14},{9,15},{10,... | collective-permute-start | bytes 442376 | tf_op jit(solution)/shard_map/ppermute | solution.py:12
  309.6 10.0 %collective-permute-start.16 = (f32[1,144,256]{2,1,0:T(8,128)S(1)}, f32[1,144,256]{2,1,0:T(8,128)S(1)}, u32[]{:S(2)}, u32[]{:S(2)}) collective-permute-start(f32[1,144,256]{2,1,0:T(8,128)S(1)} %reshape.231), channel_id=1, source_target_pairs={{0,7},{1,6},{2,5},{3,4},{4,3},{5,2},{6,1},{7,0},{8,15},{9,14},{10,... | collective-permute-start | bytes 442376 | tf_op jit(solution)/shard_map/ppermute | solution.py:12
  345.8 2.9 collective-permute-start.17
  348.7 28.1 %collective-permute-start.18 = (f32[12,12,16,128]{3,2,0,1:T(8,128)S(1)}, f32[12,12,16,128]{3,2,0,1:T(8,128)}, u32[]{:S(2)}, u32[]{:S(2)}) collective-permute-start(f32[12,12,16,128]{3,2,0,1:T(8,128)S(1)} %collective-permute-done.17), channel_id=1, source_target_pairs={{0,8},{8,0},{16,24},{24,16},{1,9},{9,1},{17,25},{25,17},{2,10},{10... | collective-permute-start | bytes 3538952 | tf_op jit(solution)/shard_map/ppermute | solution.py:12
  377.0 28.6 %collective-permute-start.19 = (f32[12,12,16,128]{3,2,0,1:T(8,128)S(1)}, f32[12,12,16,128]{3,2,0,1:T(8,128)}, u32[]{:S(2)}, u32[]{:S(2)}) collective-permute-start(f32[12,12,16,128]{3,2,0,1:T(8,128)S(1)} %broadcast_select_fusion.2), channel_id=1, source_target_pairs={{0,64},{32,96},{64,0},{96,32},{1,65},{33,97},{65,1},{97,33},{2,66}... | collective-permute-start | bytes 3538952 | tf_op jit(solution)/shard_map/ppermute | solution.py:12
  405.6 29.3 %collective-permute-start.20 = (f32[12,12,16,128]{3,2,0,1:T(8,128)}, f32[12,12,16,128]{3,2,0,1:T(8,128)S(1)}, u32[]{:S(2)}, u32[]{:S(2)}) collective-permute-start(f32[12,12,16,128]{3,2,0,1:T(8,128)} %collective-permute-done.19), channel_id=1, source_target_pairs={{0,16},{8,24},{16,0},{24,8},{1,17},{9,25},{17,1},{25,9},{2,18},{10... | collective-permute-start | bytes 3538952 | tf_op jit(solution)/shard_map/ppermute | solution.py:12
Sparse Core Ops, SparseCore 0:
  10.2 96.0 all-gather.1

commit v6 on v5

--- a/solution.py
+++ b/solution.py
@@ -78,20 +78,23 @@
     theirs = lax.dynamic_slice_in_dim(reduced_y, (1 - zh) * width, width, axis=2)
     shares = mine + shifted(theirs, "slab", lambda s: s ^ 1)
 
+    n_row = lax.axis_size("row")
+    n_col = lax.axis_size("col")
     i_n, j_n, a_n, b_n = shares.shape
     gathered = jnp.zeros((n_slab, j_n * i_n, a_n * a_n), shares.dtype)
     for d in range(n_slab):
         tile = lax.dynamic_slice_in_dim(shares, (slab_at ^ d) * a_n, a_n, axis=3)
         flat = jnp.transpose(tile, (1, 0, 3, 2)).reshape(1, j_n * i_n, a_n * a_n)
-        if d:
-            flat = shifted(flat, "slab", lambda t, d=d: t ^ d)
+        pairs = [
+            ((r * n_col + c) * n_slab + t, (c * n_col + r) * n_slab + (t ^ d))
+            for r in range(n_row)
+            for c in range(n_col)
+            for t in range(n_slab)
+        ]
+        flat = lax.ppermute(flat, ("row", "col", "slab"), pairs)
         gathered = lax.dynamic_update_slice_in_dim(gathered, flat, slab_at ^ d, axis=0)
     gathered = gathered.reshape(n_slab, j_n, i_n, a_n, a_n)
-    mirrored = jnp.transpose(gathered, (1, 2, 3, 0, 4)).reshape(j_n, i_n, a_n, b_n)
-    for bit_no in range(lax.axis_size("row").bit_length() - 1):
-        across = shifted(shifted(mirrored, "row", lambda r: r ^ 2**bit_no), "col", lambda c: c ^ 2**bit_no)
-        differ = row_at // 2**bit_no % 2 != col_at // 2**bit_no % 2
-        mirrored = jnp.where(differ, across, mirrored)
+    mirrored = jnp.transpose(gathered, (1, 2, 3, 0, 4)).reshape(shares.shape)
     return (shares + mirrored).astype(jnp.bfloat16)
 
 

time: 444 us -> 363 us (0.82)
  waiting for transfers between devices: 233 us -> 162 us
  local copies, waits for them, and re-layouts: 106 us -> 98.9 us
    ppermute x21 -> x10, waiting for transfers between devices: 229 us -> 146 us  [shifted(): lax.ppermute(value, axis, [(src, fn(src) % size) for src in range(size)])]
    ppermute x21 -> x10, starting transfers between devices: 37.6 us -> 17.6 us  [shifted(): lax.ppermute(value, axis, [(src, fn(src) % size) for src in range(size)])]
    ppermute x0 -> x8, starting transfers between devices: none -> 17.1 us  [body(): flat = lax.ppermute(flat, ('row', 'col', 'slab'), pairs)]
    ppermute x0 -> x8, waiting for transfers between devices: none -> 12.1 us  [body(): flat = lax.ppermute(flat, ('row', 'col', 'slab'), pairs)]
    dynamic_update_slice x8, local copies, waits for them, and re-layouts: 9.88 us -> 4.68 us  [body(): lax.dynamic_update_slice_in_dim(gathered, flat, slab_at ^ d, axis=0)]
  transfers between devices with their start and end apart: 22 -> 19, of which waited for: 12 -> 9; matrix products, arithmetic and copies ran while one was open for 19% -> 22% of each run, Pallas kernels for 0% -> 0%
where the time goes in v6:
time: 363 us; the launch traced here: 362 us
  waiting for transfers between devices  162 us (45%)
  local copies, waits for them, and re-layouts  98.9 us (27%)
  starting transfers between devices  34.7 us (10%)
  other arithmetic  30.2 us (8%)
  matrix products  19.7 us (5%)
  between operations  15.8 us (4%)
    ppermute x10, waiting for transfers between devices, shifted(): lax.ppermute(value, axis, [(src, fn(src) % size) for src in range(size)])  146 us
    transpose x9, local copies, waits for them, and re-layouts, body(): flat = jnp.transpose(tile, (1, 0, 3, 2)).reshape(1, j_n * i_n, a_n * a_n)  23.2 us
    dot_general x1, matrix products, body(): jnp.einsum('ikca,kcjb->ijab', amp_all, int_abs, preferred_element_type=jn...  19.7 us
    reshape x8, local copies, waits for them, and re-layouts, body(): flat = jnp.transpose(tile, (1, 0, 3, 2)).reshape(1, j_n * i_n, a_n * a_n)  17.6 us
    ppermute x10, starting transfers between devices, shifted(): lax.ppermute(value, axis, [(src, fn(src) % size) for src in range(size)])  17.6 us
    ppermute x8, starting transfers between devices, body(): flat = lax.ppermute(flat, ('row', 'col', 'slab'), pairs)  17.1 us
    transpose x1, local copies, waits for them, and re-layouts, body(): mirrored = jnp.transpose(gathered, (1, 2, 3, 0, 4)).reshape(shares.shape)  12.8 us
    ppermute x8, waiting for transfers between devices, body(): flat = lax.ppermute(flat, ('row', 'col', 'slab'), pairs)  12.1 us
  transfers between devices with their start and end apart: 19, of which 9 were waited for; matrix products, arithmetic and copies ran while one was open for 22% of the time, Pallas kernels for 0%

profile of v6, /device:TPU:0, one launch (start us, length us, event | category | flops | bytes accessed | tf_op | source)
XLA Modules:
  0.0 361.5 jit_solution(10785809490379298135)
XLA Ops:
  14.2 11.7 %and_select_fusion.1 = s32[128]{0:T(128)S(1)} fusion(s32[]{:T(128)} %bitcast.26, s32[]{:T(128)} %bitcast.27, s32[]{:T(128)} %bitcast.28, s32[]{:T(128)} %bitcast.29, s32[]{:T(128)} %bitcast.30, s32[]{:T(128)} %bitcast.32, s32[]{:T(128)} %bitcast.31, s32[]{:T(128)} %bitcast.3, s32[]{:T(128)} %bitcast.5, s32[]{:T(128)} %bitcast.7, s32[]{:T(128)} %bitcast.9, ...), kind=kLoop, calls=%fused_computation.74 | loop fusion | flops 8192 | bytes 588 | tf_op jit(solution)/shard_map/jit(_take)/select_n | solution.py:19
  27.6 3.7 %collective-permute-start.1 = (bf16[12,60,12,128]{3,1,2,0:T(8,128)(2,1)}, bf16[12,60,12,128]{3,1,2,0:T(8,128)(2,1)}, u32[]{:S(2)}, u32[]{:S(2)}) collective-permute-start(bf16[12,60,12,128]{3,1,2,0:T(8,128)(2,1)} %broadcast_select_fusion.1), channel_id=1, source_target_pairs={{0,64},{32,96},{64,0},{96,32},{1,65},{33,97},{65,1},{97,33},{2,66}... | collective-permute-start | bytes 6635528 | tf_op jit(solution)/shard_map/ppermute | solution.py:12
  31.3 51.6 %collective-permute-done.1 = bf16[12,60,12,128]{3,1,2,0:T(8,128)(2,1)} collective-permute-done((bf16[12,60,12,128]{3,1,2,0:T(8,128)(2,1)}, bf16[12,60,12,128]{3,1,2,0:T(8,128)(2,1)}, u32[]{:S(2)}, u32[]{:S(2)}) %collective-permute-start.1) | collective-permute-done | bytes 2211872 | tf_op jit(solution)/shard_map/ppermute | solution.py:12
  82.8 6.0 %broadcast_in_dim.35 = bf16[48,60,12,128]{3,1,0,2:T(8,128)(2,1)} broadcast(bf16[]{:T(256)} %constant.145.clone.1), dimensions={} | broadcast | bytes 8847362 | tf_op jit(solution)/shard_map/broadcast_in_dim | solution.py:29
  91.0 3.8 %copy_dynamic-update-slice_fusion.2 = bf16[48,60,12,128]{3,1,0,2:T(8,128)(2,1)} fusion(bf16[48,60,12,128]{3,1,0,2:T(8,128)(2,1)} %copy_dynamic-update-slice_fusion.3, s32[]{:T(128)S(6)} %select_n.264, bf16[12,60,12,128]{3,1,2,0:T(8,128)(2,1)} %collective-permute-done), kind=kLoop, calls=%fused_computation.11 | loop fusion | bytes 4718596 | tf_op jit(solution)/shard_map/dynamic_update_slice | solution.py:31
  94.8 3.8 %copy_dynamic-update-slice_fusion.1 = bf16[48,60,12,128]{3,1,0,2:T(8,128)(2,1)} fusion(bf16[48,60,12,128]{3,1,0,2:T(8,128)(2,1)} %copy_dynamic-update-slice_fusion.2, s32[]{:T(128)S(6)} %select_n.265, bf16[12,60,12,128]{3,1,2,0:T(8,128)(2,1)} %collective-permute-done.1), kind=kLoop, calls=%fused_computation.10 | loop fusion | bytes 4718596 | tf_op jit(solution)/shard_map/dynamic_update_slice | solution.py:31
  98.6 3.7 %copy_dynamic-update-slice_fusion = bf16[48,60,12,128]{3,1,0,2:T(8,128)(2,1)} fusion(bf16[48,60,12,128]{3,1,0,2:T(8,128)(2,1)} %copy_dynamic-update-slice_fusion.1, s32[]{:T(128)S(6)} %select_n.266, bf16[12,60,12,128]{3,1,2,0:T(8,128)(2,1)} %collective-permute-done.2), kind=kLoop, calls=%fused_computation.9 | loop fusion | bytes 4718596 | tf_op jit(solution)/shard_map/dynamic_update_slice | solution.py:31
  102.3 3.9 %all-gather.2.cloned.1.call-done = bf16[12,48,60,128]{3,2,1,0:T(8,128)(2,1)} async-done(((bf16[12,12,60,128]{3,2,1,0:T(8,128)(2,1)}), bf16[12,48,60,128]{3,2,1,0:T(8,128)(2,1)}) %all-gather.2.cloned.1.call-update) | async-done | bytes 8847376 | tf_op jit(solution)/shard_map/all_gather | solution.py:70
  106.3 19.7 %fusion.3 = f32[12,12,128,128]{3,2,0,1:T(8,128)S(1)} fusion(bf16[12,48,60,128]{3,2,1,0:T(8,128)(2,1)} %all-gather.2.cloned.1.call-done, bf16[48,60,12,128]{3,1,0,2:T(8,128)(2,1)} %copy_dynamic-update-slice_fusion), kind=kOutput, calls=%fused_computation.4 | convolution fusion | flops 13589544960 | bytes 27131904 | tf_op jit(solution)/shard_map/ikca,kcjb->ijab/dot_general | solution.py:72
  126.0 3.2 fusion.16
  131.4 3.0 collective-permute-start.6
  136.0 23.5 %collective-permute-done.6 = f32[6,12,32,128]{3,2,0,1:T(8,128)S(1)} collective-permute-done((f32[6,12,32,128]{3,2,0,1:T(8,128)S(1)}, f32[6,12,32,128]{3,2,0,1:T(8,128)S(1)}, u32[]{:S(2)}, u32[]{:S(2)}) %collective-permute-start.6) | collective-permute-done | bytes 1179680 | tf_op jit(solution)/shard_map/ppermute | solution.py:12
  161.0 3.8 %collective-permute-start.7 = (f32[6,12,32,128]{3,2,0,1:T(8,128)S(1)}, f32[6,12,32,128]{3,2,0,1:T(8,128)S(1)}, u32[]{:S(2)}, u32[]{:S(2)}) collective-permute-start(f32[6,12,32,128]{3,2,0,1:T(8,128)S(1)} %dynamic-slice_add_fusion.2), channel_id=1, source_target_pairs={{0,6},{1,7},{2,0},{3,1},{4,2},{5,3},{6,4},{7,5},{8,14},{9,15},{10,... | collective-permute-start | bytes 3538952 | tf_op jit(solution)/shard_map/ppermute | solution.py:12
  166.9 22.1 %collective-permute-done.7 = f32[6,12,32,128]{3,2,0,1:T(8,128)S(1)} collective-permute-done((f32[6,12,32,128]{3,2,0,1:T(8,128)S(1)}, f32[6,12,32,128]{3,2,0,1:T(8,128)S(1)}, u32[]{:S(2)}, u32[]{:S(2)}) %collective-permute-start.7) | collective-permute-done | bytes 1179680 | tf_op jit(solution)/shard_map/ppermute | solution.py:12
  190.5 3.8 %collective-permute-start.8 = (f32[6,12,32,128]{3,2,0,1:T(8,128)S(1)}, f32[6,12,32,128]{3,2,0,1:T(8,128)S(1)}, u32[]{:S(2)}, u32[]{:S(2)}) collective-permute-start(f32[6,12,32,128]{3,2,0,1:T(8,128)S(1)} %dynamic-slice_add_fusion.1), channel_id=1, source_target_pairs={{0,6},{1,7},{2,0},{3,1},{4,2},{5,3},{6,4},{7,5},{8,14},{9,15},{10,... | collective-permute-start | bytes 3538952 | tf_op jit(solution)/shard_map/ppermute | solution.py:12
  194.5 2.9 dynamic-slice_add_fusion.4
  197.5 20.2 %collective-permute-done.8 = f32[6,12,32,128]{3,2,0,1:T(8,128)S(1)} collective-permute-done((f32[6,12,32,128]{3,2,0,1:T(8,128)S(1)}, f32[6,12,32,128]{3,2,0,1:T(8,128)S(1)}, u32[]{:S(2)}, u32[]{:S(2)}) %collective-permute-start.8) | collective-permute-done | bytes 1179680 | tf_op jit(solution)/shard_map/ppermute | solution.py:12
  219.2 5.4 %collective-permute-done.5 = f32[6,12,32,128]{3,2,0,1:T(8,128)} collective-permute-done((f32[6,12,32,128]{3,2,0,1:T(8,128)}, f32[6,12,32,128]{3,2,0,1:T(8,128)}, u32[]{:S(2)}, u32[]{:S(2)}) %collective-permute-start.5) | collective-permute-done | bytes 1179680 | tf_op jit(solution)/shard_map/ppermute | solution.py:12
  226.6 3.2 collective-permute-start.9
  229.8 23.2 %collective-permute-done.9 = f32[12,12,16,128]{3,2,0,1:T(8,128)} collective-permute-done((f32[12,12,16,128]{3,2,0,1:T(8,128)S(1)}, f32[12,12,16,128]{3,2,0,1:T(8,128)}, u32[]{:S(2)}, u32[]{:S(2)}) %collective-permute-start.9) | collective-permute-done | bytes 1179680 | tf_op jit(solution)/shard_map/ppermute | solution.py:12
  254.5 5.4 %dynamic-slice_bitcast_fusion = (f32[12,12,16,16]{2,3,1,0:T(8,128)S(1)}, f32[12,12,16,16]{2,3,1,0:T(8,128)S(1)}, f32[12,12,16,16]{2,3,1,0:T(8,128)}, f32[12,12,1...) fusion(f32[12,12,16,128]{3,2,0,1:T(8,128)S(1)} %fusion.10, ...), kind=kLoop, calls=%fused_computation.19 | loop fusion | bytes 2359328 | tf_op jit(solution)/shard_map/transpose | solution.py:87
  259.9 2.7 copy.14
  265.0 2.8 collective-permute-start.10
  267.8 2.7 copy.15
  272.8 3.2 collective-permute-start.11
  276.0 2.7 copy.16
  303.1 6.1 %collective-permute-start.15 = (f32[1,144,256]{2,1,0:T(8,128)}, f32[1,144,256]{2,1,0:T(8,128)S(1)}, u32[]{:S(2)}, u32[]{:S(2)}) collective-permute-start(f32[1,144,256]{2,1,0:T(8,128)} %reshape.229), channel_id=1, source_target_pairs={{0,5},{1,4},{2,7},{3,6},{4,1},{5,0},{6,3},{7,2},{8,37},{9,36},{10,... | collective-permute-start | bytes 442376 | tf_op jit(solution)/shard_map/ppermute | solution.py:94
  311.3 3.1 collective-permute-start.17
  317.3 12.1 %collective-permute-done.16 = f32[1,144,256]{2,1,0:T(8,128)S(1)} collective-permute-done((f32[1,144,256]{2,1,0:T(8,128)S(1)}, f32[1,144,256]{2,1,0:T(8,128)S(1)}, u32[]{:S(2)}, u32[]{:S(2)}) %collective-permute-start.16) | collective-permute-done | bytes 147488 | tf_op jit(solution)/shard_map/ppermute | solution.py:94
  329.4 5.2 %reshape.232 = f32[8,12,12,16,16]{4,3,2,1,0:T(8,128)} reshape(f32[8,144,256]{2,1,0:T(8,128)S(1)} %constant_dynamic-update-slice_fusion) | data formatting | bytes 2359296 | tf_op jit(solution)/shard_map/reshape | solution.py:96
  334.6 12.8 %copy.22 = f32[12,12,16,8,16]{4,3,2,0,1:T(8,128)} copy(f32[12,12,16,8,16]{4,2,1,0,3:T(8,128)} %bitcast.153) | data formatting | bytes 2359296 | tf_op jit(solution)/shard_map/transpose | solution.py:97
  347.3 6.2 %reshape.233 = f32[12,12,16,128]{3,2,0,1:T(8,128)S(1)} reshape(f32[12,12,16,8,16]{4,3,2,0,1:T(8,128)} %copy.22) | data formatting | bytes 2359296 | tf_op jit(solution)/shard_map/reshape | solution.py:97
  (76 shorter events, 58.7 us)
Async XLA Ops:
  6.5 99.7 %all-gather.2.cloned.1.call-start = ((), (), s32[]{:S(2)}) async-start(), calls=%async_computation | async-start | bytes 11796480 | tf_op jit(solution)/shard_map/all_gather | solution.py:70
  10.0 0.7 copy-start
  10.0 16.0 %copy-start.2 = (bf16[12,60,12,128]{3,1,2,0:T(8,128)(2,1)S(1)}, bf16[12,60,12,128]{3,1,2,0:T(8,128)(2,1)}, u32[]{:S(2)}) copy-start(bf16[12,60,12,128]{3,1,2,0:T(8,128)(2,1)} %param.5) | copy-start | bytes 6635524
  27.6 55.2 %collective-permute-start.1 = (bf16[12,60,12,128]{3,1,2,0:T(8,128)(2,1)}, bf16[12,60,12,128]{3,1,2,0:T(8,128)(2,1)}, u32[]{:S(2)}, u32[]{:S(2)}) collective-permute-start(bf16[12,60,12,128]{3,1,2,0:T(8,128)(2,1)} %broadcast_select_fusion.1), channel_id=1, source_target_pairs={{0,64},{32,96},{64,0},{96,32},{1,65},{33,97},{65,1},{97,33},{2,66}... | collective-permute-start | bytes 6635528 | tf_op jit(solution)/shard_map/ppermute | solution.py:12
  31.3 59.7 %collective-permute-start = (bf16[12,60,12,128]{3,1,2,0:T(8,128)(2,1)}, bf16[12,60,12,128]{3,1,2,0:T(8,128)(2,1)}, u32[]{:S(2)}, u32[]{:S(2)}) collective-permute-start(bf16[12,60,12,128]{3,1,2,0:T(8,128)(2,1)} %broadcast_select_fusion.1), channel_id=1, source_target_pairs={{0,32},{32,0},{64,96},{96,64},{1,33},{33,1},{65,97},{97,65},{2,34}... | collective-permute-start | bytes 6635528 | tf_op jit(solution)/shard_map/ppermute | solution.py:12
  82.8 15.8 %collective-permute-start.2 = (bf16[12,60,12,128]{3,1,2,0:T(8,128)(2,1)}, bf16[12,60,12,128]{3,1,2,0:T(8,128)(2,1)}, u32[]{:S(2)}, u32[]{:S(2)}) collective-permute-start(bf16[12,60,12,128]{3,1,2,0:T(8,128)(2,1)} %collective-permute-done.1), channel_id=1, source_target_pairs={{0,32},{32,0},{64,96},{96,64},{1,33},{33,1},{65,97},{97,65},{2,34}... | collective-permute-start | bytes 6635528 | tf_op jit(solution)/shard_map/ppermute | solution.py:12
  129.2 2.2 copy-start.1
  131.4 28.1 %collective-permute-start.6 = (f32[6,12,32,128]{3,2,0,1:T(8,128)S(1)}, f32[6,12,32,128]{3,2,0,1:T(8,128)S(1)}, u32[]{:S(2)}, u32[]{:S(2)}) collective-permute-start(f32[6,12,32,128]{3,2,0,1:T(8,128)S(1)} %constant_dynamic-slice_fusion), channel_id=1, source_target_pairs={{0,6},{1,7},{2,0},{3,1},{4,2},{5,3},{6,4},{7,5},{8,14},{9,15},{10,... | collective-permute-start | bytes 3538952 | tf_op jit(solution)/shard_map/ppermute | solution.py:12
  135.9 28.9 %collective-permute-start.3 = (f32[6,12,32,128]{3,2,0,1:T(8,128)S(1)}, f32[6,12,32,128]{3,2,0,1:T(8,128)}, u32[]{:S(2)}, u32[]{:S(2)}) collective-permute-start(f32[6,12,32,128]{3,2,0,1:T(8,128)S(1)} %constant_dynamic-slice_fusion.1), channel_id=1, source_target_pairs={{0,2},{1,3},{2,4},{3,5},{4,6},{5,7},{6,0},{7,1},{8,10},{9,11},{10,... | collective-permute-start | bytes 3538952 | tf_op jit(solution)/shard_map/ppermute | solution.py:12
  161.0 28.0 %collective-permute-start.7 = (f32[6,12,32,128]{3,2,0,1:T(8,128)S(1)}, f32[6,12,32,128]{3,2,0,1:T(8,128)S(1)}, u32[]{:S(2)}, u32[]{:S(2)}) collective-permute-start(f32[6,12,32,128]{3,2,0,1:T(8,128)S(1)} %dynamic-slice_add_fusion.2), channel_id=1, source_target_pairs={{0,6},{1,7},{2,0},{3,1},{4,2},{5,3},{6,4},{7,5},{8,14},{9,15},{10,... | collective-permute-start | bytes 3538952 | tf_op jit(solution)/shard_map/ppermute | solution.py:12
  166.7 27.8 %collective-permute-start.4 = (f32[6,12,32,128]{3,2,0,1:T(8,128)S(1)}, f32[6,12,32,128]{3,2,0,1:T(8,128)}, u32[]{:S(2)}, u32[]{:S(2)}) collective-permute-start(f32[6,12,32,128]{3,2,0,1:T(8,128)S(1)} %dynamic-slice_add_fusion.5), channel_id=1, source_target_pairs={{0,2},{1,3},{2,4},{3,5},{4,6},{5,7},{6,0},{7,1},{8,10},{9,11},{10,... | collective-permute-start | bytes 3538952 | tf_op jit(solution)/shard_map/ppermute | solution.py:12
  190.5 27.1 %collective-permute-start.8 = (f32[6,12,32,128]{3,2,0,1:T(8,128)S(1)}, f32[6,12,32,128]{3,2,0,1:T(8,128)S(1)}, u32[]{:S(2)}, u32[]{:S(2)}) collective-permute-start(f32[6,12,32,128]{3,2,0,1:T(8,128)S(1)} %dynamic-slice_add_fusion.1), channel_id=1, source_target_pairs={{0,6},{1,7},{2,0},{3,1},{4,2},{5,3},{6,4},{7,5},{8,14},{9,15},{10,... | collective-permute-start | bytes 3538952 | tf_op jit(solution)/shard_map/ppermute | solution.py:12
  197.5 27.1 %collective-permute-start.5 = (f32[6,12,32,128]{3,2,0,1:T(8,128)}, f32[6,12,32,128]{3,2,0,1:T(8,128)}, u32[]{:S(2)}, u32[]{:S(2)}) collective-permute-start(f32[6,12,32,128]{3,2,0,1:T(8,128)} %dynamic-slice_add_fusion.4), channel_id=1, source_target_pairs={{0,2},{1,3},{2,4},{3,5},{4,6},{5,7},{6,0},{7,1},{8,10},{9,11},{10,... | collective-permute-start | bytes 3538952 | tf_op jit(solution)/shard_map/ppermute | solution.py:12
  226.6 26.4 %collective-permute-start.9 = (f32[12,12,16,128]{3,2,0,1:T(8,128)S(1)}, f32[12,12,16,128]{3,2,0,1:T(8,128)}, u32[]{:S(2)}, u32[]{:S(2)}) collective-permute-start(f32[12,12,16,128]{3,2,0,1:T(8,128)S(1)} %fusion.8), channel_id=1, source_target_pairs={{0,1},{1,0},{2,3},{3,2},{4,5},{5,4},{6,7},{7,6},{8,9},{9,8},{10,11... | collective-permute-start | bytes 3538952 | tf_op jit(solution)/shard_map/ppermute | solution.py:12
  265.0 38.2 %collective-permute-start.10 = (f32[1,144,256]{2,1,0:T(8,128)}, f32[1,144,256]{2,1,0:T(8,128)}, u32[]{:S(2)}, u32[]{:S(2)}) collective-permute-start(f32[1,144,256]{2,1,0:T(8,128)} %reshape.224), channel_id=1, source_target_pairs={{0,0},{1,1},{2,2},{3,3},{4,4},{5,5},{6,6},{7,7},{8,32},{9,33},{10,... | collective-permute-start | bytes 442376 | tf_op jit(solution)/shard_map/ppermute | solution.py:94
  272.8 37.5 %collective-permute-start.11 = (f32[1,144,256]{2,1,0:T(8,128)}, f32[1,144,256]{2,1,0:T(8,128)}, u32[]{:S(2)}, u32[]{:S(2)}) collective-permute-start(f32[1,144,256]{2,1,0:T(8,128)} %reshape.225), channel_id=1, source_target_pairs={{0,1},{1,0},{2,3},{3,2},{4,5},{5,4},{6,7},{7,6},{8,33},{9,32},{10,... | collective-permute-start | bytes 442376 | tf_op jit(solution)/shard_map/ppermute | solution.py:94
  281.0 30.3 %collective-permute-start.12 = (f32[1,144,256]{2,1,0:T(8,128)}, f32[1,144,256]{2,1,0:T(8,128)}, u32[]{:S(2)}, u32[]{:S(2)}) collective-permute-start(f32[1,144,256]{2,1,0:T(8,128)} %reshape.226), channel_id=1, source_target_pairs={{0,2},{1,3},{2,0},{3,1},{4,6},{5,7},{6,4},{7,5},{8,34},{9,35},{10,... | collective-permute-start | bytes 442376 | tf_op jit(solution)/shard_map/ppermute | solution.py:94
  286.0 29.3 %collective-permute-start.13 = (f32[1,144,256]{2,1,0:T(8,128)}, f32[1,144,256]{2,1,0:T(8,128)}, u32[]{:S(2)}, u32[]{:S(2)}) collective-permute-start(f32[1,144,256]{2,1,0:T(8,128)} %reshape.227), channel_id=1, source_target_pairs={{0,3},{1,2},{2,1},{3,0},{4,7},{5,6},{6,5},{7,4},{8,35},{9,34},{10,... | collective-permute-start | bytes 442376 | tf_op jit(solution)/shard_map/ppermute | solution.py:94
  292.9 23.4 %collective-permute-start.14 = (f32[1,144,256]{2,1,0:T(8,128)}, f32[1,144,256]{2,1,0:T(8,128)}, u32[]{:S(2)}, u32[]{:S(2)}) collective-permute-start(f32[1,144,256]{2,1,0:T(8,128)} %reshape.228), channel_id=1, source_target_pairs={{0,4},{1,5},{2,6},{3,7},{4,0},{5,1},{6,2},{7,3},{8,36},{9,37},{10,... | collective-permute-start | bytes 442376 | tf_op jit(solution)/shard_map/ppermute | solution.py:94
  303.1 7.2 %copy-start.4 = (f32[1,144,256]{2,1,0:T(8,128)S(1)}, f32[1,144,256]{2,1,0:T(8,128)}, u32[]{:S(2)}) copy-start(f32[1,144,256]{2,1,0:T(8,128)} %reshape.230) | copy-start | bytes 442372
  303.1 8.2 %copy-start.3 = (f32[1,144,256]{2,1,0:T(8,128)S(1)}, f32[1,144,256]{2,1,0:T(8,128)}, u32[]{:S(2)}) copy-start(f32[1,144,256]{2,1,0:T(8,128)} %reshape.231) | copy-start | bytes 442372
  303.1 14.1 %collective-permute-start.15 = (f32[1,144,256]{2,1,0:T(8,128)}, f32[1,144,256]{2,1,0:T(8,128)S(1)}, u32[]{:S(2)}, u32[]{:S(2)}) collective-permute-start(f32[1,144,256]{2,1,0:T(8,128)} %reshape.229), channel_id=1, source_target_pairs={{0,5},{1,4},{2,7},{3,6},{4,1},{5,0},{6,3},{7,2},{8,37},{9,36},{10,... | collective-permute-start | bytes 442376 | tf_op jit(solution)/shard_map/ppermute | solution.py:94
  310.3 19.1 %collective-permute-start.16 = (f32[1,144,256]{2,1,0:T(8,128)S(1)}, f32[1,144,256]{2,1,0:T(8,128)S(1)}, u32[]{:S(2)}, u32[]{:S(2)}) collective-permute-start(f32[1,144,256]{2,1,0:T(8,128)S(1)} %copy-done.4), channel_id=1, source_target_pairs={{0,6},{1,7},{2,4},{3,5},{4,2},{5,3},{6,0},{7,1},{8,38},{9,39},{10,... | collective-permute-start | bytes 442376 | tf_op jit(solution)/shard_map/ppermute | solution.py:94
  311.3 18.0 %collective-permute-start.17 = (f32[1,144,256]{2,1,0:T(8,128)S(1)}, f32[1,144,256]{2,1,0:T(8,128)S(1)}, u32[]{:S(2)}, u32[]{:S(2)}) collective-permute-start(f32[1,144,256]{2,1,0:T(8,128)S(1)} %copy-done.3), channel_id=1, source_target_pairs={{0,7},{1,6},{2,5},{3,4},{4,3},{5,2},{6,1},{7,0},{8,39},{9,38},{10,... | collective-permute-start | bytes 442376 | tf_op jit(solution)/shard_map/ppermute | solution.py:94
Sparse Core Ops, SparseCore 0:
  10.2 96.0 all-gather.1
